TPU v7x, 256 devices: a whole 4x4x8 slice. The times are simulated.
256 devices in a mesh: tm: 16 (over y_lo, z), chan: 16 (over y_hi, x, core).
Axes of the slice: x: 4, y: 4 (y_hi: 2, y_lo: 2; y = y_hi * 2 + y_lo), z: 8, core: 2. Of those that a mesh axis runs over, the one named last changes fastest.
Arguments:
- record: bfloat16 [5120, 16384], P('chan', 'tm'), may hold values from -200 to 200
- owner: int32 [4], replicated, may hold values from 0 to 15, as said below
- offsets: int32 [4, 16], replicated, may hold values from 0 to 924
Outputs:
- score: float32 [4, 16, 16384], P(None, None, 'tm')
Inputs may be any that keep to these rules, and one draw needn't show every extreme that they name: `owner`: no two batches share a time block, and one batch is always held by the last block. `offsets`: a template lies wholly inside its owner's block.
All inputs are finite; a program needn't handle non-finite values.
Results may differ from a plain program's by a relative error of at most 0.0003.
Values may be sent and summed in bfloat16 or wider, within the bound.
No kernel may reach another device: no remote copies, remote signals or barrier semaphores. Data moves between devices by JAX's collectives and lax.ppermute only.
A program may use at most 64 MiB of HBM per device.

v0:
```python
import jax
import jax.numpy as jnp
from jax import lax
from jax.sharding import PartitionSpec as P

L = 100


def from_behind(value, axis, by):
    peers = lax.axis_size(axis)
    pairs = [(i, i + by) for i in range(peers) if 0 <= i + by < peers]
    return lax.ppermute(value, axis, pairs)


def spread(value, axis, root):
    mine = lax.axis_index(axis) == root
    return lax.psum(jnp.where(mine, value, jnp.zeros_like(value)), axis)


def cut_windows(source, starts, taps):
    count = starts.shape[0]
    width = source.shape[0]
    pieces = jax.vmap(lambda s: lax.dynamic_slice_in_dim(source, s, taps, 1))(starts)
    return jnp.swapaxes(pieces, 1, 2).reshape(count, taps * width)


def correlate(weights, extended, taps, samples):
    width = extended.shape[0]
    group = 4

    def group_step(g, acc):
        stack = jnp.concatenate(
            [lax.dynamic_slice_in_dim(extended, g * group + i, samples, 1) for i in range(group)],
            axis=0,
        )
        part_weights = lax.dynamic_slice_in_dim(weights, g * group * width, group * width, 1)
        return acc + jnp.dot(part_weights, stack, preferred_element_type=jnp.float32)

    start_acc = jnp.zeros((weights.shape[0], samples), jnp.float32)
    return lax.fori_loop(0, taps // group, group_step, start_acc)


def on_device(record, owner, offsets):
    width, samples = record.shape
    batches, per_batch = offsets.shape
    taps = L
    rim = from_behind(record[:, : taps - 1], "tm", -1)
    extended = jnp.concatenate([record, rim], axis=1)
    batch_weights = []
    for b in range(batches):
        local_cut = cut_windows(record, offsets[b], taps)
        weights = spread(local_cut, "tm", owner[b])
        batch_weights.append(weights)
    all_weights = jnp.concatenate(batch_weights, axis=0)
    corr_part = correlate(all_weights, extended, taps, samples)
    widened = extended.astype(jnp.float32)
    squares = jnp.sum(widened * widened, axis=0)
    running = jnp.concatenate([jnp.zeros((1,), jnp.float32), jnp.cumsum(squares)])
    energy_part = running[taps : taps + samples] - running[:samples]
    floats = all_weights.astype(jnp.float32)
    tnorm_part = jnp.sum(floats * floats, axis=1)
    corr, energy, tnorm = lax.psum((corr_part, energy_part, tnorm_part), "chan")
    score = corr / jnp.sqrt((energy[None, :] + 1e-05) * tnorm[:, None])
    return score.reshape(batches, per_batch, samples)


def solution(mesh):
    in_specs = (P("chan", "tm"), P(), P())
    out_specs = P(None, None, "tm")
    return jax.shard_map(
        on_device, mesh=mesh, in_specs=in_specs, out_specs=out_specs, check_vma=False
    )
```

profile of v0, /device:TPU:1, one launch (start us, length us, event | category | flops | bytes accessed | tf_op | source)
XLA Modules:
  0.0 514.2 jit_solution(5866445121543216742)
XLA Ops:
  9.1 19.9 %while.20 = (s32[]{:T(128)}, bf16[320,1024]{1,0:T(8,128)(2,1)S(1)}, s32[16,2]{0,1:T(2,128)S(1)}, bf16[16,320,100]{2,1,0:T(8,128)(2,1)S(1)}, s32[]{:T(128)}) while((s32[]{:T(128)}, bf16[320,1024]{1,0:T(8,128)(2,1)S(1)}, s32[16,2]{0,1:T(2,128)S(1)}, bf16[16,320,100]{2,1,0:T(8,128)(2,1)S(1)}, s32[]{:T(128)}) %tuple.115), condition=%wide.while_cond, body=%wide.while_body.sunk | while | flops 2 | bytes 163937 | solution.py:23
  33.1 22.0 %while.21 = (s32[]{:T(128)}, bf16[320,1024]{1,0:T(8,128)(2,1)S(1)}, s32[16,2]{0,1:T(2,128)S(1)}, bf16[16,320,100]{2,1,0:T(8,128)(2,1)S(1)}, s32[]{:T(128)}) while((s32[]{:T(128)}, bf16[320,1024]{1,0:T(8,128)(2,1)S(1)}, s32[16,2]{0,1:T(2,128)S(1)}, bf16[16,320,100]{2,1,0:T(8,128)(2,1)S(1)}, s32[]{:T(128)}) %tuple.116), condition=%wide.while_cond.1, body=%wide.while_body.1.sunk | while | flops 2 | bytes 163937 | solution.py:23
  58.5 22.0 %while.22 = (s32[]{:T(128)}, bf16[320,1024]{1,0:T(8,128)(2,1)S(1)}, s32[16,2]{0,1:T(2,128)S(1)}, bf16[16,320,100]{2,1,0:T(8,128)(2,1)S(1)}, s32[]{:T(128)}) while((s32[]{:T(128)}, bf16[320,1024]{1,0:T(8,128)(2,1)S(1)}, s32[16,2]{0,1:T(2,128)S(1)}, bf16[16,320,100]{2,1,0:T(8,128)(2,1)S(1)}, s32[]{:T(128)}) %tuple.117), condition=%wide.while_cond.2, body=%wide.while_body.2.sunk | while | flops 2 | bytes 163937 | solution.py:23
  84.0 22.0 %while.23 = (s32[]{:T(128)}, bf16[320,1024]{1,0:T(8,128)(2,1)S(1)}, s32[16,2]{0,1:T(2,128)S(1)}, bf16[16,320,100]{2,1,0:T(8,128)(2,1)S(1)}, s32[]{:T(128)}) while((s32[]{:T(128)}, bf16[320,1024]{1,0:T(8,128)(2,1)S(1)}, s32[16,2]{0,1:T(2,128)S(1)}, bf16[16,320,100]{2,1,0:T(8,128)(2,1)S(1)}, s32[]{:T(128)}) %tuple.118), condition=%wide.while_cond.3, body=%wide.while_body.3.sunk | while | flops 2 | bytes 163937 | solution.py:23
  110.0 4.8 collective-permute-done
  115.7 141.9 %all-reduce.12.cloned.1.call-done = (bf16[16,32000]{1,0:T(8,128)(2,1)}, bf16[16,32000]{1,0:T(8,128)(2,1)}, bf16[16,32000]{1,0:T(8,128)(2,1)}, bf16[16,32000]{1,0:T(8,128)(2,1)}) async-done(((bf16[16,32000]{1,0:T(8,128)(2,1)}, bf16[16,32000]{1,0:T(8,128)(2,1)}, bf16[16,32000]{1,0:T(8,128)(2,1)}, bf16[16,32000]{1,0:T(8,128)(2,1)}), (bf16[16,32000]{1,0:T(8,128)(2,1)}, bf16[16,32000]{1,0:T(8,128)(2,1)}, ...) | async-done | bytes 4096016 | tf_op jit(solution)/shard_map/psum | solution.py:17
  262.5 93.8 %while.24 = (s32[]{:T(128)}, f32[64,1024]{1,0:T(8,128)}, bf16[64,32000]{1,0:T(8,128)(2,1)}, bf16[320,1123]{1,0:T(8,128)(2,1)S(1)}, s32[]{:T(128)}, /*index=5*/s3...) while((s32[]{:T(128)}, f32[64,1024]{1,0:T(8,128)}, ...), condition=%wide.region_5.6_spmd.clone, body=%wide.region_4.5_spmd.clone.sunk | while | flops 178389008 | bytes 8552849 | solution.py:40
  271.4 2.3 fusion.21
  275.1 2.3 fusion.21
  278.9 2.3 fusion.21
  282.6 2.3 fusion.21
  290.1 2.3 fusion.21
  293.9 2.3 fusion.21
  297.6 2.3 fusion.21
  301.4 2.3 fusion.21
  305.2 2.3 fusion.21
  323.9 2.3 fusion.21
  327.7 2.3 fusion.21
  331.5 2.3 fusion.21
  350.2 2.3 fusion.21
  354.0 2.3 fusion.21
  356.4 3.1 multiply_reduce_fusion
  359.4 42.8 %all-reduce.5 = (f32[64]{0:T(128)S(1)}, f32[1024]{0:T(1024)S(1)}) all-reduce(f32[64]{0:T(128)S(1)} %multiply_reduce_fusion, f32[1024]{0:T(1024)S(1)} %fusion.14), channel_id=1, replica_groups=mesh['tm'=16,'chan'=16] {'chan'}, use_global_device_ids=true, to_apply=%region_12.13 | all-reduce | flops 1088 | bytes 8704 | tf_op jit(solution)/shard_map/psum | solution.py:62
  402.2 103.4 %all-reduce.10.cloned.1.call-done = f32[64,1024]{1,0:T(8,128)} async-done(((f32[64,1024]{1,0:T(8,128)}), f32[64,1024]{1,0:T(8,128)}) %all-reduce.10.cloned.1.call-update) | async-done | bytes 262160 | tf_op jit(solution)/shard_map/psum | solution.py:62
  (283 shorter events, 168.0 us)
Async XLA Ops:
  6.5 2.6 copy-start
  6.5 251.1 %all-reduce.12.cloned.1.call-start = ((), (), s32[]{:S(2)}) async-start(), calls=%async_computation.1 | async-start | bytes 8192000 | tf_op jit(solution)/shard_map/psum | solution.py:17
  108.6 397.1 %all-reduce.10.cloned.1.call-start = ((), (), s32[]{:S(2)}) async-start(), calls=%async_computation | async-start | bytes 524288 | tf_op jit(solution)/shard_map/psum | solution.py:62
  108.6 6.2 %collective-permute-start = (bf16[320,99]{1,0:T(8,128)(2,1)S(1)}, bf16[320,99]{1,0:T(8,128)(2,1)S(1)}, u32[]{:S(2)}, u32[]{:S(2)}) collective-permute-start(bf16[320,99]{1,0:T(8,128)(2,1)S(1)} %slice.52), channel_id=1, source_target_pairs={{16,0},{32,16},{48,32},{64,48},{80,64},{96,80},{112,96},{128,112},... | collective-permute-start | bytes 190088 | tf_op jit(solution)/shard_map/ppermute | solution.py:12
  257.6 1.5 copy-start.4
  259.0 1.3 copy-start.3
  259.2 1.4 copy-start.2
  260.6 1.9 copy-start.1
Sparse Core Ops, SparseCore 0:
  108.7 148.8 all-reduce.11
  356.5 149.1 all-reduce.9
where the time goes:
time: 516 us; the launch traced here: 514 us
  waiting for transfers between devices  250 us (48%)
  local copies, waits for them, and re-layouts  138 us (27%)
  matrix products  57.9 us (11%)
  blocking collectives  42.8 us (8%)
  between operations  16.2 us (3%)
  other arithmetic  6.65 us (1%)
    psum x1, waiting for transfers between devices, spread(): return lax.psum(jnp.where(mine, value, jnp.zeros_like(value)), axis)  142 us
    psum x1, waiting for transfers between devices, on_device(): corr, energy, tnorm = lax.psum((corr_part, energy_part, tnorm_part), 'chan')  103 us
    gather x192, local copies, waits for them, and re-layouts  84.6 us
    dot_general x25, matrix products, group_step(): jnp.dot(part_weights, stack, preferred_element_type=jnp.float32)  57.9 us
    psum x1, blocking collectives, on_device(): corr, energy, tnorm = lax.psum((corr_part, energy_part, tnorm_part), 'chan')  42.8 us
    dynamic_slice x25, local copies, waits for them, and re-layouts, group_step(): lax.dynamic_slice_in_dim(extended, g * group + i, samples, 1)  35.4 us
  transfers between devices with their start and end apart: 3, of which 3 were waited for; matrix products, arithmetic and copies ran while one was open for 1% of the time, Pallas kernels for 0%

commit v1 on v0

v1 whole, which is shorter than its diff:
```python
import jax
import jax.numpy as jnp
from jax import lax
from jax.sharding import PartitionSpec as P

L = 100


def from_behind(value, axis, by):
    peers = lax.axis_size(axis)
    pairs = [(i, i + by) for i in range(peers) if 0 <= i + by < peers]
    return lax.ppermute(value, axis, pairs)


def dense_pieces(block, peers):
    size = block.size // peers
    return block.reshape(peers, 16, size // 16)


def owner_blocks(record, owner, axis):
    peers = lax.axis_size(axis)
    width, samples = record.shape
    batches = owner.shape[0]
    pieces = dense_pieces(record, peers)
    got = lax.all_to_all(pieces, axis, 0, 0, tiled=False)
    sel = jnp.stack([lax.dynamic_index_in_dim(got, owner[b], 0, keepdims=False) for b in range(batches)])
    rep = jnp.broadcast_to(sel[None], (peers,) + sel.shape)
    recv = lax.all_to_all(rep, axis, 0, 0, tiled=False)
    return jnp.swapaxes(recv, 0, 1).reshape(batches, width, samples)


def cut_windows(blocks, offsets, taps):
    batches, per_batch = offsets.shape
    _, width, samples = blocks.shape
    idx = (offsets[:, :, None] + jnp.arange(taps, dtype=offsets.dtype)[None, None, :]).reshape(batches, per_batch * taps)
    hot = (jnp.arange(samples, dtype=offsets.dtype)[None, :, None] == idx[:, None, :]).astype(blocks.dtype)
    cut = jnp.einsum("bcs,bsn->bcn", blocks, hot, preferred_element_type=jnp.float32).astype(blocks.dtype)
    cut = cut.reshape(batches, width, per_batch, taps)
    return jnp.transpose(cut, (0, 2, 1, 3)).reshape(batches * per_batch, width, taps)


def chan_sum(x, axis):
    peers = lax.axis_size(axis)
    shape = x.shape
    pieces = dense_pieces(x, peers)
    got = lax.all_to_all(pieces, axis, 0, 0, tiled=False)
    mine = jnp.sum(got, axis=0)
    rep = jnp.broadcast_to(mine[None], (peers,) + mine.shape)
    back = lax.all_to_all(rep, axis, 0, 0, tiled=False)
    return back.reshape(shape)


def on_device(record, owner, offsets):
    width, samples = record.shape
    batches, per_batch = offsets.shape
    taps = L
    templates = batches * per_batch
    rim = from_behind(record[:, : taps - 1], "tm", -1)
    extended = jnp.concatenate([record, rim], axis=1)
    blocks = owner_blocks(record, owner, "tm")
    weights = cut_windows(blocks, offsets, taps)
    corr_part = lax.conv_general_dilated(
        extended[None], weights, (1,), "VALID",
        dimension_numbers=("NCH", "OIH", "NCH"), preferred_element_type=jnp.float32,
    )[0]
    widened = extended.astype(jnp.float32)
    squares = jnp.sum(widened * widened, axis=0)
    running = jnp.concatenate([jnp.zeros((1,), jnp.float32), jnp.cumsum(squares)])
    energy_part = running[taps : taps + samples] - running[:samples]
    floats = weights.astype(jnp.float32)
    tnorm_part = jnp.sum(floats * floats, axis=(1, 2))
    rows = 80
    packed = jnp.zeros((rows, samples), jnp.float32)
    packed = packed.at[:templates].set(corr_part)
    packed = packed.at[templates].set(energy_part)
    packed = packed.at[templates + 1, :templates].set(tnorm_part)
    total = chan_sum(packed, "chan")
    corr = total[:templates]
    energy = total[templates]
    tnorm = total[templates + 1, :templates]
    score = corr / jnp.sqrt((energy[None, :] + 1e-05) * tnorm[:, None])
    return score.reshape(batches, per_batch, samples)


def solution(mesh):
    in_specs = (P("chan", "tm"), P(), P())
    out_specs = P(None, None, "tm")
    return jax.shard_map(
        on_device, mesh=mesh, in_specs=in_specs, out_specs=out_specs, check_vma=False
    )
```

time: 516 us -> 207 us (0.40)
  waiting for transfers between devices: 250 us -> 64.4 us
  local copies, waits for them, and re-layouts: 138 us -> 47.4 us
  matrix products: 57.9 us -> 32.9 us
  starting transfers between devices: 1.34 us -> 17.2 us
  blocking collectives: 42.8 us -> 31 us
  between operations: 16.2 us -> 7.77 us
    psum x2 -> x0, waiting for transfers between devices: 245 us -> none  [the longest x1 142 us: spread(): return lax.psum(jnp.where(mine, value, jnp.zeros_like(value)), axis)]
    gather x192 -> x0, local copies, waits for them, and re-layouts: 84.6 us -> none
    ppermute x1, waiting for transfers between devices: 4.84 us -> 56.1 us  [from_behind(): return lax.ppermute(value, axis, pairs)]
    dot_general x25 -> x1, matrix products: 57.9 us -> 7.54 us  [cut_windows(): jnp.einsum('bcs,bsn->bcn', blocks, hot, preferred_element_type=jnp.float32)]
    psum x1 -> x0, blocking collectives: 42.8 us -> none  [on_device(): corr, energy, tnorm = lax.psum((corr_part, energy_part, tnorm_part), 'chan')]
    dynamic_slice x25 -> x1, local copies, waits for them, and re-layouts: 35.4 us -> 0.01 us  [owner_blocks(): lax.dynamic_index_in_dim(got, owner[b], 0, keepdims=False)]
    all_to_all x0 -> x2, blocking collectives: none -> 31 us  [the longest x1 17.7 us: chan_sum(): got = lax.all_to_all(pieces, axis, 0, 0, tiled=False)]
    conv_general_dilated x0 -> x1, matrix products: none -> 25.4 us  [on_device(): lax.conv_general_dilated(extended[None], weights, (1,), 'VALID', dimensio...]
  transfers between devices with their start and end apart: 3 -> 3, of which waited for: 3 -> 2; matrix products, arithmetic and copies ran while one was open for 1% -> 6% of each run, Pallas kernels for 0% -> 0%
where the time goes in v1:
time: 207 us; the launch traced here: 206 us
  waiting for transfers between devices  64.4 us (31%)
  local copies, waits for them, and re-layouts  47.4 us (23%)
  matrix products  32.9 us (16%)
  blocking collectives  31 us (15%)
  starting transfers between devices  17.2 us (8%)
  between operations  7.77 us (4%)
  other arithmetic  5.49 us (3%)
    ppermute x1, waiting for transfers between devices, from_behind(): return lax.ppermute(value, axis, pairs)  56.1 us
    conv_general_dilated x1, matrix products, on_device(): lax.conv_general_dilated(extended[None], weights, (1,), 'VALID', dimensio...  25.4 us
    all_to_all x1, blocking collectives, chan_sum(): got = lax.all_to_all(pieces, axis, 0, 0, tiled=False)  17.7 us
    reshape x1, local copies, waits for them, and re-layouts, cut_windows(): cut = cut.reshape(batches, width, per_batch, taps)  13.4 us
    all_to_all x1, blocking collectives, chan_sum(): back = lax.all_to_all(rep, axis, 0, 0, tiled=False)  13.3 us
    all_to_all x1, starting transfers between devices, owner_blocks(): got = lax.all_to_all(pieces, axis, 0, 0, tiled=False)  10.1 us
    transpose x1, local copies, waits for them, and re-layouts, cut_windows(): jnp.transpose(cut, (0, 2, 1, 3)).reshape(batches * per_batch, width, taps)  9.51 us
    all_to_all x1, waiting for transfers between devices, owner_blocks(): got = lax.all_to_all(pieces, axis, 0, 0, tiled=False)  8.3 us
  transfers between devices with their start and end apart: 3, of which 2 were waited for; matrix products, arithmetic and copies ran while one was open for 6% of the time, Pallas kernels for 0%

profile of v1, /device:TPU:1, one launch (start us, length us, event | category | flops | bytes accessed | tf_op | source)
XLA Modules:
  0.0 206.2 jit_solution(9312669307112520610)
XLA Ops:
  0.0 2.4 %reshape.137 = bf16[16,16,1280]{2,1,0:T(8,128)(2,1)} reshape(bf16[320,1024]{1,0:T(8,128)(2,1)} %param.9) | data formatting | bytes 1310720 | tf_op jit(solution)/shard_map/reshape | solution.py:17
  2.4 10.1 %all-to-all-start = ((bf16[16,16,1280]{2,1,0:T(8,128)(2,1)}), bf16[16,16,1280]{2,1,0:T(8,128)(2,1)S(1)}, u32[]{:S(2)}, u32[]{:S(2)}) async-start(bf16[16,16,1280]{2,1,0:T(8,128)(2,1)} %reshape.137), calls=%async_computation | async-start | bytes 1310720 | tf_op jit(solution)/shard_map/all_to_all | solution.py:25
  12.6 1.4 fusion.19
  21.6 8.3 %all-to-all-done = bf16[16,16,1280]{2,1,0:T(8,128)(2,1)S(1)} async-done(((bf16[16,16,1280]{2,1,0:T(8,128)(2,1)}), bf16[16,16,1280]{2,1,0:T(8,128)(2,1)S(1)}, u32[]{:S(2)}, u32[]{:S(2)}) %all-to-all-start) | async-done | bytes 655392 | tf_op jit(solution)/shard_map/all_to_all | solution.py:25
  30.0 1.8 broadcast_in_dim.7
  31.7 5.8 %all-to-all-start.1 = ((bf16[16,4,16,1280]{3,2,1,0:T(8,128)(2,1)}), bf16[16,4,16,1280]{3,2,1,0:T(8,128)(2,1)S(1)}, u32[]{:S(2)}, u32[]{:S(2)}) async-start(bf16[16,4,16,1280]{3,2,1,0:T(8,128)(2,1)} %broadcast_in_dim.7), calls=%async_computation.1 | async-start | bytes 5242880 | tf_op jit(solution)/shard_map/all_to_all | solution.py:28
  37.5 0.9 slice.91
  38.4 1.3 collective-permute-start
  40.0 1.1 constant_dynamic-update-slice_fusion.1
  41.1 56.1 %collective-permute-done = bf16[320,99]{1,0:T(8,128)(2,1)S(1)} collective-permute-done((bf16[320,99]{1,0:T(8,128)(2,1)S(1)}, bf16[320,99]{1,0:T(8,128)(2,1)S(1)}, u32[]{:S(2)}, u32[]{:S(2)}) %collective-permute-start) | collective-permute-done | bytes 63392 | tf_op jit(solution)/shard_map/ppermute | solution.py:12
  97.8 0.9 pad.12
  98.7 3.8 %reshape.161 = bf16[320,1,8,141]{3,2,0,1:T(8,128)(2,1)} reshape(bf16[320,1,1128]{2,0,1:T(8,128)(2,1)} %pad.12) | data formatting | bytes 1443840 | tf_op jit(solution)/shard_map/conv_general_dilated | solution.py:62
  102.5 2.7 %copy.16 = bf16[320,1,8,141]{0,2,3,1:T(8,128)(2,1)S(1)} copy(bf16[320,1,8,141]{3,2,0,1:T(8,128)(2,1)} %reshape.161) | data formatting | bytes 1443840 | tf_op jit(solution)/shard_map/conv_general_dilated | solution.py:62
  105.2 1.0 slice.106
  106.4 1.8 copy.17
  108.2 4.5 %reshape.138 = bf16[4,320,1024]{2,1,0:T(8,128)(2,1)S(1)} reshape(bf16[4,16,16,1280]{3,2,1,0:T(8,128)(2,1)} %copy.17) | data formatting | bytes 5242880 | tf_op jit(solution)/shard_map/reshape | solution.py:29
  112.7 7.5 %fusion.2 = bf16[4,320,1600]{2,1,0:T(8,128)(2,1)} fusion(bf16[4,320,1024]{2,1,0:T(8,128)(2,1)S(1)} %reshape.138, s32[4,1600]{1,0:T(4,128)S(1)} %broadcast_add_fusion), kind=kOutput, calls=%fused_computation.4 | convolution fusion | flops 4202905600 | bytes 6743040 | tf_op jit(solution)/shard_map/bcs,bsn->bcn/dot_general | solution.py:37
  120.3 13.4 %reshape.139 = bf16[4,320,16,100]{3,2,1,0:T(8,128)(2,1)} reshape(bf16[4,320,1600]{2,1,0:T(8,128)(2,1)} %fusion.2) | data formatting | bytes 8192000 | tf_op jit(solution)/shard_map/reshape | solution.py:38
  133.7 4.0 %multiply_reduce_fusion = f32[4,16]{1,0:T(4,128)S(1)} fusion(bf16[4,320,16,100]{3,2,1,0:T(8,128)(2,1)} %reshape.139), kind=kLoop, calls=%fused_computation.3 | loop fusion | flops 6143936 | bytes 4096256 | tf_op jit(solution)/shard_map/reduce_sum | solution.py:71
  137.7 9.5 %copy.18 = bf16[4,16,320,100]{2,1,0,3:T(8,128)(2,1)} copy(bf16[4,16,320,100]{3,1,2,0:T(8,128)(2,1)} %bitcast.36) | data formatting | bytes 8192000 | tf_op jit(solution)/shard_map/transpose | solution.py:39
  147.2 25.4 %fusion.11 = f32[8,141,64]{2,0,1:T(8,128)S(1)} fusion(bf16[64,320,100]{1,0,2:T(8,128)(2,1)} %bitcast.39, bf16[320,1,7,99]{0,2,3,1:T(8,128)(2,1)S(1)} %copy-done, bf16[320,1,8,141]{0,2,3,1:T(8,128)(2,1)S(1)} %copy.16, pred[8,141]{0,1:T(8,128)(4,1)S(1)} %copy-done.2), kind=kOutput, calls=%fused_computation.14 | convolution fusion | flops 4624046592 | bytes 5551336 | tf_op jit(solution)/shard_map/conv_general_dilated | solution.py:62
  174.0 17.7 %all_to_all.20 = f32[16,16,320]{2,1,0:T(8,128)S(1)} all-to-all(f32[16,16,320]{2,1,0:T(8,128)S(1)} %reshape.146), channel_id=1, replica_groups=mesh['tm'=16,'chan'=16] {'chan'}, dimensions={0} | all-to-all | bytes 655360 | tf_op jit(solution)/shard_map/all_to_all | solution.py:46
  191.8 13.3 %all_to_all.21 = f32[16,16,320]{2,1,0:T(8,128)S(1)} all-to-all(f32[16,16,320]{2,1,0:T(8,128)S(1)} %broadcast_in_dim.8), channel_id=1, replica_groups=mesh['tm'=16,'chan'=16] {'chan'}, dimensions={0} | all-to-all | bytes 655360 | tf_op jit(solution)/shard_map/all_to_all | solution.py:49
  205.4 0.8 slice_multiply_fusion
  (36 shorter events, 2.9 us)
Async XLA Ops:
  2.4 27.5 %all-to-all-start = ((bf16[16,16,1280]{2,1,0:T(8,128)(2,1)}), bf16[16,16,1280]{2,1,0:T(8,128)(2,1)S(1)}, u32[]{:S(2)}, u32[]{:S(2)}) async-start(bf16[16,16,1280]{2,1,0:T(8,128)(2,1)} %reshape.137), calls=%async_computation | async-start | bytes 1310720 | tf_op jit(solution)/shard_map/all_to_all | solution.py:25
  31.7 8.1 %copy-start.1 = (s32[4,16]{1,0:T(4,128)S(1)}, s32[4,16]{1,0:T(4,128)}, u32[]{:S(2)}) copy-start(s32[4,16]{1,0:T(4,128)} %param.11) | copy-start | bytes 772
  31.7 74.7 %all-to-all-start.1 = ((bf16[16,4,16,1280]{3,2,1,0:T(8,128)(2,1)}), bf16[16,4,16,1280]{3,2,1,0:T(8,128)(2,1)S(1)}, u32[]{:S(2)}, u32[]{:S(2)}) async-start(bf16[16,4,16,1280]{3,2,1,0:T(8,128)(2,1)} %broadcast_in_dim.7), calls=%async_computation.1 | async-start | bytes 5242880 | tf_op jit(solution)/shard_map/all_to_all | solution.py:28
  38.4 58.8 %collective-permute-start = (bf16[320,99]{1,0:T(8,128)(2,1)S(1)}, bf16[320,99]{1,0:T(8,128)(2,1)S(1)}, u32[]{:S(2)}, u32[]{:S(2)}) collective-permute-start(bf16[320,99]{1,0:T(8,128)(2,1)S(1)} %slice.91), channel_id=1, source_target_pairs={{16,0},{32,16},{48,32},{64,48},{80,64},{96,80},{112,96},{128,112},... | collective-permute-start | bytes 190088 | tf_op jit(solution)/shard_map/ppermute | solution.py:12
  137.7 9.5 %copy-start = (bf16[320,1,7,99]{0,2,3,1:T(8,128)(2,1)S(1)}, bf16[320,1,7,99]{0,2,3,1:T(8,128)(2,1)}, u32[]{:S(2)}) copy-start(bf16[320,1,7,99]{0,2,3,1:T(8,128)(2,1)} %slice.106) | copy-start | bytes 1330564
  137.7 9.5 %copy-start.2 = (pred[8,141]{0,1:T(8,128)(4,1)S(1)}, pred[8,141]{0,1:T(8,128)(4,1)}, u32[]{:S(2)}) copy-start(pred[8,141]{0,1:T(8,128)(4,1)} %constant.112) | copy-start | bytes 3388

commit v2 on v1

--- a/solution.py
+++ b/solution.py
@@ -4,6 +4,7 @@
 from jax.sharding import PartitionSpec as P
 
 L = 100
+PHASES = 4
 
 
 def from_behind(value, axis, by):
@@ -29,14 +30,24 @@
     return jnp.swapaxes(recv, 0, 1).reshape(batches, width, samples)
 
 
-def cut_windows(blocks, offsets, taps):
+def cut_windows(blocks, offsets, taps, phases):
     batches, per_batch = offsets.shape
     _, width, samples = blocks.shape
-    idx = (offsets[:, :, None] + jnp.arange(taps, dtype=offsets.dtype)[None, None, :]).reshape(batches, per_batch * taps)
-    hot = (jnp.arange(samples, dtype=offsets.dtype)[None, :, None] == idx[:, None, :]).astype(blocks.dtype)
-    cut = jnp.einsum("bcs,bsn->bcn", blocks, hot, preferred_element_type=jnp.float32).astype(blocks.dtype)
-    cut = cut.reshape(batches, width, per_batch, taps)
-    return jnp.transpose(cut, (0, 2, 1, 3)).reshape(batches * per_batch, width, taps)
+    steps = taps // phases
+    lag = jnp.arange(taps, dtype=offsets.dtype).reshape(steps, phases)
+    idx = offsets[:, :, None, None] + lag[None, None]
+    hot = (jnp.arange(samples, dtype=offsets.dtype) == idx[..., None]).astype(blocks.dtype)
+    cut = jnp.einsum("bkips,bcs->ibkpc", hot, blocks, preferred_element_type=jnp.float32).astype(blocks.dtype)
+    return cut.reshape(steps, batches * per_batch * phases, width)
+
+
+def window_norms(blocks, offsets, taps):
+    floats = blocks.astype(jnp.float32)
+    column = jnp.sum(floats * floats, axis=1)
+    samples = blocks.shape[2]
+    at = jnp.arange(samples, dtype=offsets.dtype)
+    inside = (at >= offsets[:, :, None]) & (at < offsets[:, :, None] + taps)
+    return jnp.sum(jnp.where(inside, column[:, None, :], 0.0), axis=2).reshape(-1)
 
 
 def chan_sum(x, axis):
@@ -58,17 +69,21 @@
     rim = from_behind(record[:, : taps - 1], "tm", -1)
     extended = jnp.concatenate([record, rim], axis=1)
     blocks = owner_blocks(record, owner, "tm")
-    weights = cut_windows(blocks, offsets, taps)
-    corr_part = lax.conv_general_dilated(
-        extended[None], weights, (1,), "VALID",
-        dimension_numbers=("NCH", "OIH", "NCH"), preferred_element_type=jnp.float32,
+    phases = PHASES
+    weights = cut_windows(blocks, offsets, taps, phases)
+    out = lax.conv_general_dilated(
+        extended[None], weights, (1,), "VALID", rhs_dilation=(phases,),
+        dimension_numbers=("NCH", "HOI", "NCH"), preferred_element_type=jnp.float32,
     )[0]
+    out = out.reshape(templates, phases, out.shape[-1])
+    corr_part = out[:, 0, :samples]
+    for p in range(1, phases):
+        corr_part = corr_part + out[:, p, p : p + samples]
     widened = extended.astype(jnp.float32)
     squares = jnp.sum(widened * widened, axis=0)
     running = jnp.concatenate([jnp.zeros((1,), jnp.float32), jnp.cumsum(squares)])
     energy_part = running[taps : taps + samples] - running[:samples]
-    floats = weights.astype(jnp.float32)
-    tnorm_part = jnp.sum(floats * floats, axis=(1, 2))
+    tnorm_part = window_norms(blocks, offsets, taps)
     rows = 80
     packed = jnp.zeros((rows, samples), jnp.float32)
     packed = packed.at[:templates].set(corr_part)

time: 207 us -> 174 us (0.84)
  local copies, waits for them, and re-layouts: 47.4 us -> 28.4 us
  matrix products: 32.9 us -> 16.9 us
    conv_general_dilated x1, matrix products: 25.4 us -> 6.27 us  [on_device(): lax.conv_general_dilated(extended[None], weights, (1,), 'VALID', rhs_dila...]
    reshape x1 -> x0, local copies, waits for them, and re-layouts: 13.4 us -> none  [cut_windows(): cut = cut.reshape(batches, width, per_batch, taps)]
    transpose x1 -> x0, local copies, waits for them, and re-layouts: 9.51 us -> none  [cut_windows(): jnp.transpose(cut, (0, 2, 1, 3)).reshape(batches * per_batch, width, taps)]
    dot_general x1, matrix products: 7.54 us -> 10.7 us  [cut_windows(): jnp.einsum('bkips,bcs->ibkpc', hot, blocks, preferred_element_type=jnp.fl...]
    add x1 -> x3, other arithmetic: 0.01 us -> 3.01 us  [the longest x1 2.21 us: on_device(): corr_part = corr_part + out[:, p, p:p + samples]]
    reshape x1 -> x2, local copies, waits for them, and re-layouts: 4.54 us -> 7.1 us  [owner_blocks(): return jnp.swapaxes(recv, 0, 1).reshape(batches, width, samples)]
    conv_general_dilated x5 -> x7, local copies, waits for them, and re-layouts: 8.1 us -> 8.39 us  [on_device(): lax.conv_general_dilated(extended[None], weights, (1,), 'VALID', rhs_dila...]
  transfers between devices with their start and end apart: 3 -> 3, of which waited for: 2 -> 2; matrix products, arithmetic and copies ran while one was open for 6% -> 7% of each run, Pallas kernels for 0% -> 0%
where the time goes in v2:
time: 174 us; the launch traced here: 173 us
  waiting for transfers between devices  64.6 us (37%)
  blocking collectives  31 us (18%)
  local copies, waits for them, and re-layouts  28.4 us (16%)
  starting transfers between devices  17.2 us (10%)
  matrix products  16.9 us (10%)
  between operations  7.83 us (4%)
  other arithmetic  7.17 us (4%)
    ppermute x1, waiting for transfers between devices, from_behind(): return lax.ppermute(value, axis, pairs)  55.5 us
    all_to_all x1, blocking collectives, chan_sum(): got = lax.all_to_all(pieces, axis, 0, 0, tiled=False)  17.7 us
    all_to_all x1, blocking collectives, chan_sum(): back = lax.all_to_all(rep, axis, 0, 0, tiled=False)  13.3 us
    dot_general x1, matrix products, cut_windows(): jnp.einsum('bkips,bcs->ibkpc', hot, blocks, preferred_element_type=jnp.fl...  10.7 us
    all_to_all x1, starting transfers between devices, owner_blocks(): got = lax.all_to_all(pieces, axis, 0, 0, tiled=False)  10.1 us
    all_to_all x1, waiting for transfers between devices, owner_blocks(): got = lax.all_to_all(pieces, axis, 0, 0, tiled=False)  9.09 us
    conv_general_dilated x7, local copies, waits for them, and re-layouts, on_device(): lax.conv_general_dilated(extended[None], weights, (1,), 'VALID', rhs_dila...  8.39 us
    reshape x2, local copies, waits for them, and re-layouts, owner_blocks(): return jnp.swapaxes(recv, 0, 1).reshape(batches, width, samples)  7.1 us
  transfers between devices with their start and end apart: 3, of which 2 were waited for; matrix products, arithmetic and copies ran while one was open for 7% of the time, Pallas kernels for 0%

profile of v2, /device:TPU:1, one launch (start us, length us, event | category | flops | bytes accessed | tf_op | source)
XLA Modules:
  0.0 173.2 jit_solution(1602292194089853692)
XLA Ops:
  0.0 2.5 %reshape.135 = bf16[16,16,1280]{2,1,0:T(8,128)(2,1)} reshape(bf16[320,1024]{1,0:T(8,128)(2,1)} %param.9) | data formatting | bytes 1310720 | tf_op jit(solution)/shard_map/reshape | solution.py:18
  2.5 10.1 %all-to-all-start = ((bf16[16,16,1280]{2,1,0:T(8,128)(2,1)}), bf16[16,16,1280]{2,1,0:T(8,128)(2,1)S(1)}, u32[]{:S(2)}, u32[]{:S(2)}) async-start(bf16[16,16,1280]{2,1,0:T(8,128)(2,1)} %reshape.135), calls=%async_computation | async-start | bytes 1310720 | tf_op jit(solution)/shard_map/all_to_all | solution.py:26
  20.8 9.1 %all-to-all-done = bf16[16,16,1280]{2,1,0:T(8,128)(2,1)S(1)} async-done(((bf16[16,16,1280]{2,1,0:T(8,128)(2,1)}), bf16[16,16,1280]{2,1,0:T(8,128)(2,1)S(1)}, u32[]{:S(2)}, u32[]{:S(2)}) %all-to-all-start) | async-done | bytes 655392 | tf_op jit(solution)/shard_map/all_to_all | solution.py:26
  30.0 1.8 %broadcast_in_dim.15 = bf16[16,4,16,1280]{3,2,1,0:T(8,128)(2,1)} broadcast(bf16[4,16,1280]{2,1,0:T(8,128)(2,1)S(1)} %pad_maximum_fusion), dimensions={1,2,3} | broadcast | bytes 2785280 | tf_op jit(solution)/shard_map/broadcast_in_dim | solution.py:28
  31.7 5.8 %all-to-all-start.1 = ((bf16[16,4,16,1280]{3,2,1,0:T(8,128)(2,1)}), bf16[16,4,16,1280]{3,2,1,0:T(8,128)(2,1)S(1)}, u32[]{:S(2)}, u32[]{:S(2)}) async-start(bf16[16,4,16,1280]{3,2,1,0:T(8,128)(2,1)} %broadcast_in_dim.15), calls=%async_computation.1 | async-start | bytes 5242880 | tf_op jit(solution)/shard_map/all_to_all | solution.py:29
  37.5 0.9 slice.103
  38.4 1.3 collective-permute-start
  40.5 1.1 constant_dynamic-update-slice_fusion.1
  41.7 55.5 %collective-permute-done = bf16[320,99]{1,0:T(8,128)(2,1)S(1)} collective-permute-done((bf16[320,99]{1,0:T(8,128)(2,1)S(1)}, bf16[320,99]{1,0:T(8,128)(2,1)S(1)}, u32[]{:S(2)}, u32[]{:S(2)}) %collective-permute-start) | collective-permute-done | bytes 63392 | tf_op jit(solution)/shard_map/ppermute | solution.py:13
  97.8 0.9 pad.12
  98.7 3.8 %reshape.159 = bf16[320,1,8,141]{3,2,0,1:T(8,128)(2,1)} reshape(bf16[320,1,1128]{2,0,1:T(8,128)(2,1)} %pad.12) | data formatting | bytes 1443840 | tf_op jit(solution)/shard_map/conv_general_dilated | solution.py:74
  102.5 2.7 %copy.20 = bf16[320,1,8,141]{0,2,3,1:T(8,128)(2,1)S(1)} copy(bf16[320,1,8,141]{3,2,0,1:T(8,128)(2,1)} %reshape.159) | data formatting | bytes 1443840 | tf_op jit(solution)/shard_map/conv_general_dilated | solution.py:74
  105.2 1.0 slice.122
  106.4 1.5 copy-done
  107.9 2.0 %copy.21 = bf16[4,16,16,1280]{3,2,1,0:T(8,128)(2,1)S(1)} copy(bf16[4,16,16,1280]{3,2,0,1:T(8,128)(2,1)} %bitcast.38) | data formatting | bytes 5242880 | tf_op jit(solution)/shard_map/transpose | solution.py:30
  109.9 3.6 %reshape.157 = bf16[4,320,1024,1,1]{2,1,0,3,4:T(8,128)(2,1)} reshape(bf16[4,16,16,1280]{3,2,1,0:T(8,128)(2,1)S(1)} %copy.21) | data formatting | bytes 5242880 | tf_op jit(solution)/shard_map/reshape | solution.py:30
  113.5 3.5 %reshape.136 = bf16[4,320,1024]{2,1,0:T(8,128)(2,1)} reshape(bf16[4,16,16,1280]{3,2,1,0:T(8,128)(2,1)S(1)} %copy.21) | data formatting | bytes 5242880 | tf_op jit(solution)/shard_map/reshape | solution.py:30
  117.0 2.5 %multiply_reduce_fusion = f32[4,1024]{1,0:T(4,128)S(1)} fusion(bf16[4,320,1024]{2,1,0:T(8,128)(2,1)} %reshape.136), kind=kLoop, calls=%fused_computation.3 | loop fusion | flops 3928064 | bytes 2637824 | tf_op jit(solution)/shard_map/reduce_sum | solution.py:46
  119.8 10.7 %fusion.4 = bf16[4,320,16,25,4]{1,3,4,2,0:T(8,128)(2,1)S(1)} fusion(s32[4,16,25,4]{2,3,1,0:T(4,128)} %broadcast_add_fusion, bf16[4,320,1024,1,1]{2,1,0,3,4:T(8,128)(2,1)S(1)} %copy-done.1), kind=kOutput, calls=%fused_computation.6 | convolution fusion | flops 4202905600 | bytes 6743040 | tf_op jit(solution)/shard_map/bkips,bcs->ibkpc/dot_general | solution.py:40
  130.5 6.3 %fusion.13 = f32[8,141,256]{2,0,1:T(8,128)S(1)} fusion(bf16[25,256,320]{2,0,1:T(8,128)(2,1)S(1)} %bitcast.44, bf16[320,1,7,96]{0,2,3,1:T(8,128)(2,1)S(1)} %copy-done.2, bf16[320,1,8,141]{0,2,3,1:T(8,128)(2,1)S(1)} %copy.20, pred[8,141]{0,1:T(8,128)(4,1)S(1)} %copy-done.5), kind=kOutput, calls=%fused_computation.16 | convolution fusion | flops 4624217088 | bytes 6404200 | tf_op jit(solution)/shard_map/conv_general_dilated | solution.py:74
  138.1 2.2 %slice_add_fusion = f32[64,1,1024]{2,1,0:T(1,128)S(1)} fusion(f32[64,4,1027]{2,1,0:T(4,128)S(1)} %reshape_squeeze.3), kind=kLoop, calls=%fused_computation.20 | loop fusion | flops 196608 | bytes 1310720 | tf_op jit(solution)/shard_map/add | solution.py:81
  141.0 17.7 %all_to_all.20 = f32[16,16,320]{2,1,0:T(8,128)S(1)} all-to-all(f32[16,16,320]{2,1,0:T(8,128)S(1)} %reshape.142), channel_id=1, replica_groups=mesh['tm'=16,'chan'=16] {'chan'}, dimensions={0} | all-to-all | bytes 655360 | tf_op jit(solution)/shard_map/all_to_all | solution.py:57
  158.8 13.3 %all_to_all.21 = f32[16,16,320]{2,1,0:T(8,128)S(1)} all-to-all(f32[16,16,320]{2,1,0:T(8,128)S(1)} %broadcast_in_dim.22), channel_id=1, replica_groups=mesh['tm'=16,'chan'=16] {'chan'}, dimensions={0} | all-to-all | bytes 655360 | tf_op jit(solution)/shard_map/all_to_all | solution.py:60
  172.4 0.8 slice_multiply_fusion
  (44 shorter events, 4.9 us)
Async XLA Ops:
  0.0 12.6 %copy-start.4 = (s32[4]{0:T(128)S(1)}, s32[4]{0:T(128)}, u32[]{:S(2)}) copy-start(s32[4]{0:T(128)} %param.10) | copy-start | bytes 52
  2.5 27.5 %all-to-all-start = ((bf16[16,16,1280]{2,1,0:T(8,128)(2,1)}), bf16[16,16,1280]{2,1,0:T(8,128)(2,1)S(1)}, u32[]{:S(2)}, u32[]{:S(2)}) async-start(bf16[16,16,1280]{2,1,0:T(8,128)(2,1)} %reshape.135), calls=%async_computation | async-start | bytes 1310720 | tf_op jit(solution)/shard_map/all_to_all | solution.py:26
  31.7 8.0 %copy-start.3 = (s32[4,16]{1,0:T(4,128)S(1)}, s32[4,16]{1,0:T(4,128)}, u32[]{:S(2)}) copy-start(s32[4,16]{1,0:T(4,128)} %param.11) | copy-start | bytes 772
  31.7 74.7 %all-to-all-start.1 = ((bf16[16,4,16,1280]{3,2,1,0:T(8,128)(2,1)}), bf16[16,4,16,1280]{3,2,1,0:T(8,128)(2,1)S(1)}, u32[]{:S(2)}, u32[]{:S(2)}) async-start(bf16[16,4,16,1280]{3,2,1,0:T(8,128)(2,1)} %broadcast_in_dim.15), calls=%async_computation.1 | async-start | bytes 5242880 | tf_op jit(solution)/shard_map/all_to_all | solution.py:29
  38.4 58.8 %collective-permute-start = (bf16[320,99]{1,0:T(8,128)(2,1)S(1)}, bf16[320,99]{1,0:T(8,128)(2,1)S(1)}, u32[]{:S(2)}, u32[]{:S(2)}) collective-permute-start(bf16[320,99]{1,0:T(8,128)(2,1)S(1)} %slice.103), channel_id=1, source_target_pairs={{16,0},{32,16},{48,32},{64,48},{80,64},{96,80},{112,96},{128,112},... | collective-permute-start | bytes 190088 | tf_op jit(solution)/shard_map/ppermute | solution.py:13
  106.4 1.5 copy-start
  117.0 2.7 %copy-start.1 = (bf16[4,320,1024,1,1]{2,1,0,3,4:T(8,128)(2,1)S(1)}, bf16[4,320,1024,1,1]{2,1,0,3,4:T(8,128)(2,1)}, u32[]{:S(2)}) copy-start(bf16[4,320,1024,1,1]{2,1,0,3,4:T(8,128)(2,1)} %reshape.157) | copy-start | bytes 7864324
  119.8 10.7 %copy-start.2 = (bf16[320,1,7,96]{0,2,3,1:T(8,128)(2,1)S(1)}, bf16[320,1,7,96]{0,2,3,1:T(8,128)(2,1)}, u32[]{:S(2)}) copy-start(bf16[320,1,7,96]{0,2,3,1:T(8,128)(2,1)} %slice.122) | copy-start | bytes 1290244
  119.8 10.7 %copy-start.5 = (pred[8,141]{0,1:T(8,128)(4,1)S(1)}, pred[8,141]{0,1:T(8,128)(4,1)}, u32[]{:S(2)}) copy-start(pred[8,141]{0,1:T(8,128)(4,1)} %constant.116) | copy-start | bytes 3388

commit v3 on v2

v3 whole, which is shorter than its diff:
```python
import jax
import jax.numpy as jnp
from jax import lax
from jax.sharding import PartitionSpec as P

L = 100
PHASES = 4
STAGES = 1


def from_behind(value, axis, by):
    peers = lax.axis_size(axis)
    pairs = [(i, i + by) for i in range(peers) if 0 <= i + by < peers]
    return lax.ppermute(value, axis, pairs)


def dense_pieces(block, peers):
    size = block.size // peers
    return block.reshape(peers, size // 128, 128)


def scatter_owners(record, owner, axis):
    peers = lax.axis_size(axis)
    pieces = dense_pieces(record, peers)
    got = lax.all_to_all(pieces, axis, 0, 0, tiled=False)
    return jnp.stack([lax.dynamic_index_in_dim(got, owner[b], 0, keepdims=False) for b in range(owner.shape[0])])


def gather_blocks(sel, axis, shape):
    peers = lax.axis_size(axis)
    rep = jnp.broadcast_to(sel[None], (peers,) + sel.shape)
    recv = lax.all_to_all(rep, axis, 0, 0, tiled=False)
    return jnp.swapaxes(recv, 0, 1).reshape((sel.shape[0],) + shape)


def cut_windows(blocks, offsets, taps, span, phases):
    batches, per_batch = offsets.shape
    _, width, samples = blocks.shape
    steps = span // phases
    lag = jnp.arange(span, dtype=offsets.dtype).reshape(steps, phases)
    idx = offsets[:, :, None, None] + lag[None, None]
    hot = (jnp.arange(samples, dtype=offsets.dtype) == idx[..., None]) & (lag[None, None, :, :, None] < taps)
    hot = hot.astype(blocks.dtype)
    cut = jnp.einsum("bkips,bcs->ibkpc", hot, blocks, preferred_element_type=jnp.float32).astype(blocks.dtype)
    return cut.reshape(steps, batches * per_batch * phases, width)


def window_norms(blocks, offsets, taps):
    floats = blocks.astype(jnp.float32)
    column = jnp.sum(floats * floats, axis=1)
    samples = blocks.shape[2]
    at = jnp.arange(samples, dtype=offsets.dtype)
    inside = (at >= offsets[:, :, None]) & (at < offsets[:, :, None] + taps)
    return jnp.sum(jnp.where(inside, column[:, None, :], 0.0), axis=2).reshape(-1)


def chan_sum(x, axis):
    peers = lax.axis_size(axis)
    shape = x.shape
    pieces = dense_pieces(x, peers)
    got = lax.all_to_all(pieces, axis, 0, 0, tiled=False)
    mine = jnp.sum(got, axis=0)
    rep = jnp.broadcast_to(mine[None], (peers,) + mine.shape)
    back = lax.all_to_all(rep, axis, 0, 0, tiled=False)
    return back.reshape(shape)


def correlate(extended, weights, phases, count, samples):
    out = lax.conv_general_dilated(
        extended[None], weights, (1,), "VALID", rhs_dilation=(phases,),
        dimension_numbers=("NCH", "HOI", "NCH"), preferred_element_type=jnp.float32,
    )[0]
    out = out.reshape(count, phases, out.shape[-1])
    corr = out[:, 0, :samples]
    for p in range(1, phases):
        corr = corr + out[:, p, p : p + samples]
    return corr


def on_device(record, owner, offsets):
    width, samples = record.shape
    batches, per_batch = offsets.shape
    taps = L
    templates = batches * per_batch
    phases = PHASES
    span = -(-taps // phases) * phases
    rim = from_behind(record[:, : taps - 1], "tm", -1)
    rim, record = lax.optimization_barrier((rim, record))
    extended = jnp.concatenate(
        [record, rim, jnp.zeros((width, span - taps), record.dtype)], axis=1
    )
    widened = extended[:, : samples + taps - 1].astype(jnp.float32)
    squares = jnp.sum(widened * widened, axis=0)
    running = jnp.concatenate([jnp.zeros((1,), jnp.float32), jnp.cumsum(squares)])
    energy_part = running[taps : taps + samples] - running[:samples]
    sel = scatter_owners(record, owner, "tm")
    step = batches // STAGES
    corrs = []
    norms = []
    for g in range(STAGES):
        part = slice(g * step, (g + 1) * step)
        blocks = gather_blocks(sel[part], "tm", (width, samples))
        weights = cut_windows(blocks, offsets[part], taps, span, phases)
        corrs.append(correlate(extended, weights, phases, step * per_batch, samples))
        norms.append(window_norms(blocks, offsets[part], taps))
    rows = 80
    packed = jnp.zeros((rows, samples), jnp.float32)
    packed = packed.at[:templates].set(jnp.concatenate(corrs, axis=0))
    packed = packed.at[templates].set(energy_part)
    packed = packed.at[templates + 1, :templates].set(jnp.concatenate(norms))
    total = chan_sum(packed, "chan")
    corr = total[:templates]
    energy = total[templates]
    tnorm = total[templates + 1, :templates]
    score = corr / jnp.sqrt((energy[None, :] + 1e-05) * tnorm[:, None])
    return score.reshape(batches, per_batch, samples)


def solution(mesh):
    in_specs = (P("chan", "tm"), P(), P())
    out_specs = P(None, None, "tm")
    return jax.shard_map(
        on_device, mesh=mesh, in_specs=in_specs, out_specs=out_specs, check_vma=False
    )
```

time: 174 us -> 169 us (0.971)
  waiting for transfers between devices: 64.6 us -> 61.5 us
    ppermute x1, waiting for transfers between devices: 55.5 us -> 4.9 us  [from_behind(): return lax.ppermute(value, axis, pairs)]
    all_to_all x2, waiting for transfers between devices: 9.1 us -> 56.6 us  [the longest x1 49.2 us: gather_blocks(): recv = lax.all_to_all(rep, axis, 0, 0, tiled=False)]
  transfers between devices with their start and end apart: 3 -> 3, of which waited for: 2 -> 3; matrix products, arithmetic and copies ran while one was open for 7% -> 7% of each run, Pallas kernels for 0% -> 0%
where the time goes in v3:
time: 169 us; the launch traced here: 168 us
  waiting for transfers between devices  61.5 us (36%)
  blocking collectives  30.2 us (18%)
  local copies, waits for them, and re-layouts  27 us (16%)
  matrix products  18.1 us (11%)
  starting transfers between devices  16.4 us (10%)
  between operations  7.84 us (5%)
  other arithmetic  7.17 us (4%)
    all_to_all x1, waiting for transfers between devices, gather_blocks(): recv = lax.all_to_all(rep, axis, 0, 0, tiled=False)  49.2 us
    all_to_all x1, blocking collectives, chan_sum(): got = lax.all_to_all(pieces, axis, 0, 0, tiled=False)  17.5 us
    all_to_all x1, blocking collectives, chan_sum(): back = lax.all_to_all(rep, axis, 0, 0, tiled=False)  12.7 us
    dot_general x1, matrix products, cut_windows(): jnp.einsum('bkips,bcs->ibkpc', hot, blocks, preferred_element_type=jnp.fl...  11.9 us
    all_to_all x1, starting transfers between devices, scatter_owners(): got = lax.all_to_all(pieces, axis, 0, 0, tiled=False)  9.12 us
    conv_general_dilated x7, local copies, waits for them, and re-layouts, correlate(): lax.conv_general_dilated(extended[None], weights, (1,), 'VALID', rhs_dila...  8.39 us
    all_to_all x1, waiting for transfers between devices, scatter_owners(): got = lax.all_to_all(pieces, axis, 0, 0, tiled=False)  7.42 us
    conv_general_dilated x1, matrix products, correlate(): lax.conv_general_dilated(extended[None], weights, (1,), 'VALID', rhs_dila...  6.27 us
  transfers between devices with their start and end apart: 3, of which 3 were waited for; matrix products, arithmetic and copies ran while one was open for 7% of the time, Pallas kernels for 0%

profile of v3, /device:TPU:1, one launch (start us, length us, event | category | flops | bytes accessed | tf_op | source)
XLA Modules:
  0.0 168.3 jit_solution(13864754142575630872)
XLA Ops:
  0.0 0.9 slice.103
  0.9 1.3 collective-permute-start
  2.2 4.9 %collective-permute-done = bf16[320,99]{1,0:T(8,128)(2,1)S(1)} collective-permute-done((bf16[320,99]{1,0:T(8,128)(2,1)S(1)}, bf16[320,99]{1,0:T(8,128)(2,1)S(1)}, u32[]{:S(2)}, u32[]{:S(2)}) %collective-permute-start) | collective-permute-done | bytes 63392 | tf_op jit(solution)/shard_map/ppermute | solution.py:14
  7.1 2.1 %reshape.147 = bf16[16,160,128]{2,1,0:T(8,128)(2,1)} reshape(bf16[320,1024]{1,0:T(8,128)(2,1)} %param.9) | data formatting | bytes 1310720 | tf_op jit(solution)/shard_map/reshape | solution.py:19
  9.2 9.1 %all-to-all-start = ((bf16[16,160,128]{2,1,0:T(8,128)(2,1)}), bf16[16,160,128]{2,1,0:T(8,128)(2,1)S(1)}, u32[]{:S(2)}, u32[]{:S(2)}) async-start(bf16[16,160,128]{2,1,0:T(8,128)(2,1)} %reshape.147), calls=%async_computation | async-start | bytes 1310720 | tf_op jit(solution)/shard_map/all_to_all | solution.py:25
  26.6 7.4 %all-to-all-done = bf16[16,160,128]{2,1,0:T(8,128)(2,1)S(1)} async-done(((bf16[16,160,128]{2,1,0:T(8,128)(2,1)}), bf16[16,160,128]{2,1,0:T(8,128)(2,1)S(1)}, u32[]{:S(2)}, u32[]{:S(2)}) %all-to-all-start) | async-done | bytes 655392 | tf_op jit(solution)/shard_map/all_to_all | solution.py:25
  34.0 2.0 %broadcast_in_dim.15 = bf16[16,4,160,128]{3,2,1,0:T(8,128)(2,1)} broadcast(bf16[4,160,128]{2,1,0:T(8,128)(2,1)S(1)} %pad_maximum_fusion), dimensions={1,2,3} | broadcast | bytes 2785280 | tf_op jit(solution)/shard_map/broadcast_in_dim | solution.py:31
  36.0 6.0 %all-to-all-start.1 = ((bf16[16,4,160,128]{3,2,1,0:T(8,128)(2,1)}), bf16[16,4,160,128]{3,2,1,0:T(8,128)(2,1)S(1)}, u32[]{:S(2)}, u32[]{:S(2)}) async-start(bf16[16,4,160,128]{3,2,1,0:T(8,128)(2,1)} %broadcast_in_dim.15), calls=%async_computation.1 | async-start | bytes 5242880 | tf_op jit(solution)/shard_map/all_to_all | solution.py:32
  42.9 1.1 constant_dynamic-update-slice_fusion.1
  44.6 0.9 pad.12
  45.5 3.8 %reshape.171 = bf16[320,1,8,141]{3,2,0,1:T(8,128)(2,1)} reshape(bf16[320,1,1128]{2,0,1:T(8,128)(2,1)} %pad.12) | data formatting | bytes 1443840 | tf_op jit(solution)/shard_map/conv_general_dilated | solution.py:69
  49.3 2.7 %copy.20 = bf16[320,1,8,141]{0,2,3,1:T(8,128)(2,1)S(1)} copy(bf16[320,1,8,141]{3,2,0,1:T(8,128)(2,1)} %reshape.171) | data formatting | bytes 1443840 | tf_op jit(solution)/shard_map/conv_general_dilated | solution.py:69
  52.0 1.0 slice.122
  53.2 49.2 %all-to-all-done.1 = bf16[16,4,160,128]{3,2,1,0:T(8,128)(2,1)S(1)} async-done(((bf16[16,4,160,128]{3,2,1,0:T(8,128)(2,1)}), bf16[16,4,160,128]{3,2,1,0:T(8,128)(2,1)S(1)}, u32[]{:S(2)}, u32[]{:S(2)}) %all-to-all-start.1) | async-done | bytes 2621472 | tf_op jit(solution)/shard_map/all_to_all | solution.py:32
  102.5 1.5 copy-done
  104.0 2.0 %copy.21 = bf16[4,16,160,128]{3,2,1,0:T(8,128)(2,1)S(1)} copy(bf16[4,16,160,128]{3,2,0,1:T(8,128)(2,1)} %bitcast.38) | data formatting | bytes 5242880 | tf_op jit(solution)/shard_map/transpose | solution.py:33
  105.9 3.1 %reshape.169 = bf16[4,320,1024,1,1]{2,1,0,3,4:T(8,128)(2,1)} reshape(bf16[4,16,160,128]{3,2,1,0:T(8,128)(2,1)S(1)} %copy.21) | data formatting | bytes 5242880 | tf_op jit(solution)/shard_map/reshape | solution.py:33
  109.0 3.1 %reshape.148 = bf16[4,320,1024]{2,1,0:T(8,128)(2,1)} reshape(bf16[4,16,160,128]{3,2,1,0:T(8,128)(2,1)S(1)} %copy.21) | data formatting | bytes 5242880 | tf_op jit(solution)/shard_map/reshape | solution.py:33
  112.2 2.5 %multiply_reduce_fusion = f32[4,1024]{1,0:T(4,128)S(1)} fusion(bf16[4,320,1024]{2,1,0:T(8,128)(2,1)} %reshape.148), kind=kLoop, calls=%fused_computation.5 | loop fusion | flops 3928064 | bytes 2637824 | tf_op jit(solution)/shard_map/reduce_sum | solution.py:50
  114.9 11.9 %fusion.7 = bf16[4,320,16,25,4]{1,3,4,2,0:T(8,128)(2,1)S(1)} fusion(s32[4,16,25,4]{2,3,1,0:T(4,128)} %broadcast_add_fusion, pred[25,4]{0,1:T(4,128)(4,1)S(1)} %broadcast_compare_fusion, bf16[4,320,1024,1,1]{2,1,0,3,4:T(8,128)(2,1)S(1)} %copy-done.1), kind=kOutput, calls=%fused_computation.8 | convolution fusion | flops 4209459200 | bytes 6743140 | tf_op jit(solution)/shard_map/bkips,bcs->ibkpc/dot_general | solution.py:44
  126.8 6.3 %fusion.18 = f32[8,141,256]{2,0,1:T(8,128)S(1)} fusion(bf16[25,256,320]{2,0,1:T(8,128)(2,1)S(1)} %bitcast.44, bf16[320,1,7,96]{0,2,3,1:T(8,128)(2,1)S(1)} %copy-done.2, bf16[320,1,8,141]{0,2,3,1:T(8,128)(2,1)S(1)} %copy.20, pred[8,141]{0,1:T(8,128)(4,1)S(1)} %copy-done.5), kind=kOutput, calls=%fused_computation.18 | convolution fusion | flops 4624217088 | bytes 6404200 | tf_op jit(solution)/shard_map/conv_general_dilated | solution.py:69
  134.4 2.2 %slice_add_fusion = f32[64,1,1024]{2,1,0:T(1,128)S(1)} fusion(f32[64,4,1027]{2,1,0:T(4,128)S(1)} %reshape_squeeze.3), kind=kLoop, calls=%fused_computation.22 | loop fusion | flops 196608 | bytes 1310720 | tf_op jit(solution)/shard_map/add | solution.py:76
  137.2 17.5 %all_to_all.20 = f32[16,40,128]{2,1,0:T(8,128)S(1)} all-to-all(f32[16,40,128]{2,1,0:T(8,128)S(1)} %reshape.154), channel_id=1, replica_groups=mesh['tm'=16,'chan'=16] {'chan'}, dimensions={0} | all-to-all | bytes 655360 | tf_op jit(solution)/shard_map/all_to_all | solution.py:61
  154.8 12.7 %all_to_all.21 = f32[16,40,128]{2,1,0:T(8,128)S(1)} all-to-all(f32[16,40,128]{2,1,0:T(8,128)S(1)} %broadcast_in_dim.22), channel_id=1, replica_groups=mesh['tm'=16,'chan'=16] {'chan'}, dimensions={0} | all-to-all | bytes 655360 | tf_op jit(solution)/shard_map/all_to_all | solution.py:64
  (45 shorter events, 5.3 us)
Async XLA Ops:
  0.0 18.3 %copy-start.4 = (s32[4]{0:T(128)S(1)}, s32[4]{0:T(128)}, u32[]{:S(2)}) copy-start(s32[4]{0:T(128)} %param.10) | copy-start | bytes 52
  0.9 6.2 %collective-permute-start = (bf16[320,99]{1,0:T(8,128)(2,1)S(1)}, bf16[320,99]{1,0:T(8,128)(2,1)S(1)}, u32[]{:S(2)}, u32[]{:S(2)}) collective-permute-start(bf16[320,99]{1,0:T(8,128)(2,1)S(1)} %slice.103), channel_id=1, source_target_pairs={{16,0},{32,16},{48,32},{64,48},{80,64},{96,80},{112,96},{128,112},... | collective-permute-start | bytes 190088 | tf_op jit(solution)/shard_map/ppermute | solution.py:14
  9.2 24.8 %all-to-all-start = ((bf16[16,160,128]{2,1,0:T(8,128)(2,1)}), bf16[16,160,128]{2,1,0:T(8,128)(2,1)S(1)}, u32[]{:S(2)}, u32[]{:S(2)}) async-start(bf16[16,160,128]{2,1,0:T(8,128)(2,1)} %reshape.147), calls=%async_computation | async-start | bytes 1310720 | tf_op jit(solution)/shard_map/all_to_all | solution.py:25
  36.0 6.0 %copy-start.3 = (s32[4,16]{1,0:T(4,128)S(1)}, s32[4,16]{1,0:T(4,128)}, u32[]{:S(2)}) copy-start(s32[4,16]{1,0:T(4,128)} %param.11) | copy-start | bytes 772
  36.0 66.4 %all-to-all-start.1 = ((bf16[16,4,160,128]{3,2,1,0:T(8,128)(2,1)}), bf16[16,4,160,128]{3,2,1,0:T(8,128)(2,1)S(1)}, u32[]{:S(2)}, u32[]{:S(2)}) async-start(bf16[16,4,160,128]{3,2,1,0:T(8,128)(2,1)} %broadcast_in_dim.15), calls=%async_computation.1 | async-start | bytes 5242880 | tf_op jit(solution)/shard_map/all_to_all | solution.py:32
  102.5 1.5 copy-start
  112.2 2.7 %copy-start.1 = (bf16[4,320,1024,1,1]{2,1,0,3,4:T(8,128)(2,1)S(1)}, bf16[4,320,1024,1,1]{2,1,0,3,4:T(8,128)(2,1)}, u32[]{:S(2)}) copy-start(bf16[4,320,1024,1,1]{2,1,0,3,4:T(8,128)(2,1)} %reshape.169) | copy-start | bytes 7864324
  114.9 11.9 %copy-start.2 = (bf16[320,1,7,96]{0,2,3,1:T(8,128)(2,1)S(1)}, bf16[320,1,7,96]{0,2,3,1:T(8,128)(2,1)}, u32[]{:S(2)}) copy-start(bf16[320,1,7,96]{0,2,3,1:T(8,128)(2,1)} %slice.122) | copy-start | bytes 1290244
  114.9 11.9 %copy-start.5 = (pred[8,141]{0,1:T(8,128)(4,1)S(1)}, pred[8,141]{0,1:T(8,128)(4,1)}, u32[]{:S(2)}) copy-start(pred[8,141]{0,1:T(8,128)(4,1)} %constant.118) | copy-start | bytes 3388

commit v4 on v3

--- a/solution.py
+++ b/solution.py
@@ -6,6 +6,8 @@
 L = 100
 PHASES = 4
 STAGES = 1
+BLOCK_GRID = (4, 4)
+SUM_GRID = (2, 8)
 
 
 def from_behind(value, axis, by):
@@ -14,14 +16,23 @@
     return lax.ppermute(value, axis, pairs)
 
 
-def dense_pieces(block, peers):
-    size = block.size // peers
-    return block.reshape(peers, size // 128, 128)
+def dense_pieces(block, across):
+    down = block.shape[0] // across[0]
+    wide = block.shape[1] // across[1]
+    grid = block.reshape(across[0], down, across[1], wide)
+    return jnp.transpose(grid, (0, 2, 1, 3)).reshape(across[0] * across[1], down, wide)
+
+
+def join_pieces(pieces, across):
+    _, *middle, down, wide = pieces.shape
+    grid = pieces.reshape(across[0], across[1], *middle, down, wide)
+    lead = len(middle)
+    order = tuple(range(2, 2 + lead)) + (0, 2 + lead, 1, 3 + lead)
+    return jnp.transpose(grid, order).reshape(*middle, across[0] * down, across[1] * wide)
 
 
 def scatter_owners(record, owner, axis):
-    peers = lax.axis_size(axis)
-    pieces = dense_pieces(record, peers)
+    pieces = dense_pieces(record, BLOCK_GRID)
     got = lax.all_to_all(pieces, axis, 0, 0, tiled=False)
     return jnp.stack([lax.dynamic_index_in_dim(got, owner[b], 0, keepdims=False) for b in range(owner.shape[0])])
 
@@ -30,7 +41,7 @@
     peers = lax.axis_size(axis)
     rep = jnp.broadcast_to(sel[None], (peers,) + sel.shape)
     recv = lax.all_to_all(rep, axis, 0, 0, tiled=False)
-    return jnp.swapaxes(recv, 0, 1).reshape((sel.shape[0],) + shape)
+    return join_pieces(recv, BLOCK_GRID)
 
 
 def cut_windows(blocks, offsets, taps, span, phases):
@@ -56,13 +67,12 @@
 
 def chan_sum(x, axis):
     peers = lax.axis_size(axis)
-    shape = x.shape
-    pieces = dense_pieces(x, peers)
+    pieces = dense_pieces(x, SUM_GRID)
     got = lax.all_to_all(pieces, axis, 0, 0, tiled=False)
     mine = jnp.sum(got, axis=0)
     rep = jnp.broadcast_to(mine[None], (peers,) + mine.shape)
     back = lax.all_to_all(rep, axis, 0, 0, tiled=False)
-    return back.reshape(shape)
+    return join_pieces(back, SUM_GRID)
 
 
 def correlate(extended, weights, phases, count, samples):

time: 169 us -> 166 us (0.982)
  other arithmetic: 7.17 us -> 5.26 us
    transpose x1 -> x3, local copies, waits for them, and re-layouts: 1.96 us -> 4.51 us  [the longest x2 3.59 us: join_pieces(): jnp.transpose(grid, order)]
    reshape x5 -> x3, local copies, waits for them, and re-layouts: 8.44 us -> 6.11 us  [the longest x1 4.24 us: join_pieces(): jnp.transpose(grid, order)]
    reduce_sum x1, other arithmetic: 2.46 us -> 0.55 us  [window_norms(): column = jnp.sum(floats * floats, axis=1)]
where the time goes in v4:
time: 166 us; the launch traced here: 165 us
  waiting for transfers between devices  61.6 us (37%)
  blocking collectives  30.2 us (18%)
  local copies, waits for them, and re-layouts  25.6 us (15%)
  matrix products  18.2 us (11%)
  starting transfers between devices  16.4 us (10%)
  between operations  7.85 us (5%)
  other arithmetic  5.26 us (3%)
    all_to_all x1, waiting for transfers between devices, gather_blocks(): recv = lax.all_to_all(rep, axis, 0, 0, tiled=False)  49.2 us
    all_to_all x1, blocking collectives, chan_sum(): got = lax.all_to_all(pieces, axis, 0, 0, tiled=False)  17.5 us
    all_to_all x1, blocking collectives, chan_sum(): back = lax.all_to_all(rep, axis, 0, 0, tiled=False)  12.7 us
    dot_general x1, matrix products, cut_windows(): jnp.einsum('bkips,bcs->ibkpc', hot, blocks, preferred_element_type=jnp.fl...  11.9 us
    all_to_all x1, starting transfers between devices, scatter_owners(): got = lax.all_to_all(pieces, axis, 0, 0, tiled=False)  9.12 us
    conv_general_dilated x7, local copies, waits for them, and re-layouts, correlate(): lax.conv_general_dilated(extended[None], weights, (1,), 'VALID', rhs_dila...  8.38 us
    all_to_all x1, waiting for transfers between devices, scatter_owners(): got = lax.all_to_all(pieces, axis, 0, 0, tiled=False)  7.42 us
    conv_general_dilated x1, matrix products, correlate(): lax.conv_general_dilated(extended[None], weights, (1,), 'VALID', rhs_dila...  6.27 us
  transfers between devices with their start and end apart: 3, of which 3 were waited for; matrix products, arithmetic and copies ran while one was open for 7% of the time, Pallas kernels for 0%

profile of v4, /device:TPU:1, one launch (start us, length us, event | category | flops | bytes accessed | tf_op | source)
XLA Modules:
  0.0 165.0 jit_solution(17815021994317637011)
XLA Ops:
  0.0 0.9 slice.103
  0.9 1.3 collective-permute-start
  2.2 4.9 %collective-permute-done = bf16[320,99]{1,0:T(8,128)(2,1)S(1)} collective-permute-done((bf16[320,99]{1,0:T(8,128)(2,1)S(1)}, bf16[320,99]{1,0:T(8,128)(2,1)S(1)}, u32[]{:S(2)}, u32[]{:S(2)}) %collective-permute-start) | collective-permute-done | bytes 63392 | tf_op jit(solution)/shard_map/ppermute | solution.py:16
  7.1 1.8 %reshape.161 = bf16[4,80,4,256]{3,2,1,0:T(4,128)(2,1)S(1)} reshape(bf16[320,1024]{1,0:T(8,128)(2,1)} %param.9) | data formatting | bytes 1310720 | tf_op jit(solution)/shard_map/reshape | solution.py:22
  8.9 0.9 copy.36
  9.8 9.1 %all-to-all-start = ((bf16[16,80,256]{2,1,0:T(8,128)(2,1)}), bf16[16,80,256]{2,1,0:T(8,128)(2,1)S(1)}, u32[]{:S(2)}, u32[]{:S(2)}) async-start(bf16[16,80,256]{2,1,0:T(8,128)(2,1)} %bitcast.3), calls=%async_computation | async-start | bytes 1310720 | tf_op jit(solution)/shard_map/all_to_all | solution.py:36
  27.2 7.4 %all-to-all-done = bf16[16,80,256]{2,1,0:T(8,128)(2,1)S(1)} async-done(((bf16[16,80,256]{2,1,0:T(8,128)(2,1)}), bf16[16,80,256]{2,1,0:T(8,128)(2,1)S(1)}, u32[]{:S(2)}, u32[]{:S(2)}) %all-to-all-start) | async-done | bytes 655392 | tf_op jit(solution)/shard_map/all_to_all | solution.py:36
  34.7 1.8 %broadcast_in_dim.17 = bf16[16,4,80,256]{3,2,1,0:T(8,128)(2,1)} broadcast(bf16[4,80,256]{2,1,0:T(8,128)(2,1)S(1)} %pad_maximum_fusion), dimensions={1,2,3} | broadcast | bytes 2785280 | tf_op jit(solution)/shard_map/broadcast_in_dim | solution.py:42
  36.4 6.0 %all-to-all-start.1 = ((bf16[16,4,80,256]{3,2,1,0:T(8,128)(2,1)}), bf16[16,4,80,256]{3,2,1,0:T(8,128)(2,1)S(1)}, u32[]{:S(2)}, u32[]{:S(2)}) async-start(bf16[16,4,80,256]{3,2,1,0:T(8,128)(2,1)} %broadcast_in_dim.17), calls=%async_computation.1 | async-start | bytes 5242880 | tf_op jit(solution)/shard_map/all_to_all | solution.py:43
  42.5 0.8 broadcast_add_fusion
  43.3 1.1 constant_dynamic-update-slice_fusion.1
  45.0 0.9 pad.12
  45.9 3.8 %reshape.189 = bf16[320,1,8,141]{3,2,0,1:T(8,128)(2,1)} reshape(bf16[320,1,1128]{2,0,1:T(8,128)(2,1)} %pad.12) | data formatting | bytes 1443840 | tf_op jit(solution)/shard_map/conv_general_dilated | solution.py:79
  49.7 2.7 %copy.35 = bf16[320,1,8,141]{0,2,3,1:T(8,128)(2,1)S(1)} copy(bf16[320,1,8,141]{3,2,0,1:T(8,128)(2,1)} %reshape.189) | data formatting | bytes 1443840 | tf_op jit(solution)/shard_map/conv_general_dilated | solution.py:79
  52.4 1.0 slice.122
  53.6 49.2 %all-to-all-done.1 = bf16[16,4,80,256]{3,2,1,0:T(8,128)(2,1)S(1)} async-done(((bf16[16,4,80,256]{3,2,1,0:T(8,128)(2,1)}), bf16[16,4,80,256]{3,2,1,0:T(8,128)(2,1)S(1)}, u32[]{:S(2)}, u32[]{:S(2)}) %all-to-all-start.1) | async-done | bytes 2621472 | tf_op jit(solution)/shard_map/all_to_all | solution.py:43
  103.4 3.5 %copy.37 = bf16[4,4,80,4,256]{4,3,2,1,0:T(4,128)(2,1)} copy(bf16[4,4,80,4,256]{4,2,0,3,1:T(8,128)(2,1)S(1)} %bitcast.54) | data formatting | bytes 5242880 | tf_op jit(solution)/shard_map/transpose | solution.py:31
  106.9 4.2 %reshape.187 = bf16[4,320,1024,1,1]{2,1,0,3,4:T(8,128)(2,1)S(1)} reshape(bf16[4,4,80,4,256]{4,3,2,1,0:T(4,128)(2,1)} %copy.37) | data formatting | bytes 5242880 | tf_op jit(solution)/shard_map/reshape | solution.py:31
  111.4 11.9 %fusion.7 = bf16[4,320,16,25,4]{1,3,4,2,0:T(8,128)(2,1)S(1)} fusion(s32[4,16,25,4]{2,3,1,0:T(4,128)} %broadcast_add_fusion, pred[25,4]{0,1:T(4,128)(4,1)S(1)} %broadcast_compare_fusion, bf16[4,320,1024,1,1]{2,1,0,3,4:T(8,128)(2,1)S(1)} %reshape.187), kind=kOutput, calls=%fused_computation.8 | convolution fusion | flops 4209459200 | bytes 6743140 | tf_op jit(solution)/shard_map/bkips,bcs->ibkpc/dot_general | solution.py:55
  123.4 6.3 %fusion.18 = f32[8,141,256]{2,0,1:T(8,128)S(1)} fusion(bf16[25,256,320]{2,0,1:T(8,128)(2,1)S(1)} %bitcast.70, bf16[320,1,7,96]{0,2,3,1:T(8,128)(2,1)S(1)} %copy-done, bf16[320,1,8,141]{0,2,3,1:T(8,128)(2,1)S(1)} %copy.35, pred[8,141]{0,1:T(8,128)(4,1)S(1)} %copy-done.3), kind=kOutput, calls=%fused_computation.18 | convolution fusion | flops 4624217088 | bytes 6404200 | tf_op jit(solution)/shard_map/conv_general_dilated | solution.py:79
  131.0 2.2 %slice_add_fusion = f32[64,1,1024]{2,1,0:T(1,128)S(1)} fusion(f32[64,4,1027]{2,1,0:T(4,128)S(1)} %reshape_squeeze.3), kind=kLoop, calls=%fused_computation.23 | loop fusion | flops 196608 | bytes 1310720 | tf_op jit(solution)/shard_map/add | solution.py:86
  133.8 17.5 %all_to_all.20 = f32[16,40,128]{2,1,0:T(8,128)S(1)} all-to-all(f32[16,40,128]{2,1,0:T(8,128)S(1)} %bitcast.59), channel_id=1, replica_groups=mesh['tm'=16,'chan'=16] {'chan'}, dimensions={0} | all-to-all | bytes 655360 | tf_op jit(solution)/shard_map/all_to_all | solution.py:71
  151.4 12.7 %all_to_all.21 = f32[16,40,128]{2,1,0:T(8,128)S(1)} all-to-all(f32[16,40,128]{2,1,0:T(8,128)S(1)} %broadcast_in_dim.25), channel_id=1, replica_groups=mesh['tm'=16,'chan'=16] {'chan'}, dimensions={0} | all-to-all | bytes 655360 | tf_op jit(solution)/shard_map/all_to_all | solution.py:74
  164.2 0.8 slice_multiply_fusion
  (43 shorter events, 4.4 us)
Async XLA Ops:
  0.0 19.0 %copy-start.2 = (s32[4]{0:T(128)S(1)}, s32[4]{0:T(128)}, u32[]{:S(2)}) copy-start(s32[4]{0:T(128)} %param.10) | copy-start | bytes 52
  0.9 6.2 %collective-permute-start = (bf16[320,99]{1,0:T(8,128)(2,1)S(1)}, bf16[320,99]{1,0:T(8,128)(2,1)S(1)}, u32[]{:S(2)}, u32[]{:S(2)}) collective-permute-start(bf16[320,99]{1,0:T(8,128)(2,1)S(1)} %slice.103), channel_id=1, source_target_pairs={{16,0},{32,16},{48,32},{64,48},{80,64},{96,80},{112,96},{128,112},... | collective-permute-start | bytes 190088 | tf_op jit(solution)/shard_map/ppermute | solution.py:16
  9.8 24.8 %all-to-all-start = ((bf16[16,80,256]{2,1,0:T(8,128)(2,1)}), bf16[16,80,256]{2,1,0:T(8,128)(2,1)S(1)}, u32[]{:S(2)}, u32[]{:S(2)}) async-start(bf16[16,80,256]{2,1,0:T(8,128)(2,1)} %bitcast.3), calls=%async_computation | async-start | bytes 1310720 | tf_op jit(solution)/shard_map/all_to_all | solution.py:36
  36.4 6.0 %copy-start.1 = (s32[4,16]{1,0:T(4,128)S(1)}, s32[4,16]{1,0:T(4,128)}, u32[]{:S(2)}) copy-start(s32[4,16]{1,0:T(4,128)} %param.11) | copy-start | bytes 772
  36.4 66.4 %all-to-all-start.1 = ((bf16[16,4,80,256]{3,2,1,0:T(8,128)(2,1)}), bf16[16,4,80,256]{3,2,1,0:T(8,128)(2,1)S(1)}, u32[]{:S(2)}, u32[]{:S(2)}) async-start(bf16[16,4,80,256]{3,2,1,0:T(8,128)(2,1)} %broadcast_in_dim.17), calls=%async_computation.1 | async-start | bytes 5242880 | tf_op jit(solution)/shard_map/all_to_all | solution.py:43
  111.4 11.9 %copy-start = (bf16[320,1,7,96]{0,2,3,1:T(8,128)(2,1)S(1)}, bf16[320,1,7,96]{0,2,3,1:T(8,128)(2,1)}, u32[]{:S(2)}) copy-start(bf16[320,1,7,96]{0,2,3,1:T(8,128)(2,1)} %slice.122) | copy-start | bytes 1290244
  111.4 11.9 %copy-start.3 = (pred[8,141]{0,1:T(8,128)(4,1)S(1)}, pred[8,141]{0,1:T(8,128)(4,1)}, u32[]{:S(2)}) copy-start(pred[8,141]{0,1:T(8,128)(4,1)} %constant.118) | copy-start | bytes 3388

commit v5 on v4

--- a/solution.py
+++ b/solution.py
@@ -95,7 +95,8 @@
     phases = PHASES
     span = -(-taps // phases) * phases
     rim = from_behind(record[:, : taps - 1], "tm", -1)
-    rim, record = lax.optimization_barrier((rim, record))
+    sel = scatter_owners(record, owner, "tm")
+    rim, sel = lax.optimization_barrier((rim, sel))
     extended = jnp.concatenate(
         [record, rim, jnp.zeros((width, span - taps), record.dtype)], axis=1
     )
@@ -103,7 +104,6 @@
     squares = jnp.sum(widened * widened, axis=0)
     running = jnp.concatenate([jnp.zeros((1,), jnp.float32), jnp.cumsum(squares)])
     energy_part = running[taps : taps + samples] - running[:samples]
-    sel = scatter_owners(record, owner, "tm")
     step = batches // STAGES
     corrs = []
     norms = []

time: 166 us -> 163 us (0.982)
  waiting for transfers between devices: 61.6 us -> 56.7 us
  starting transfers between devices: 16.4 us -> 18.9 us
    ppermute x1, waiting for transfers between devices: 4.9 us -> 0.01 us  [from_behind(): return lax.ppermute(value, axis, pairs)]
  transfers between devices with their start and end apart: 3 -> 3, of which waited for: 3 -> 2; matrix products, arithmetic and copies ran while one was open for 7% -> 8% of each run, Pallas kernels for 0% -> 0%
where the time goes in v5:
time: 163 us; the launch traced here: 162 us
  waiting for transfers between devices  56.7 us (35%)
  blocking collectives  29.7 us (18%)
  local copies, waits for them, and re-layouts  25.6 us (16%)
  starting transfers between devices  18.9 us (12%)
  matrix products  18.2 us (11%)
  between operations  7.85 us (5%)
  other arithmetic  5.26 us (3%)
    all_to_all x1, waiting for transfers between devices, gather_blocks(): recv = lax.all_to_all(rep, axis, 0, 0, tiled=False)  49.7 us
    all_to_all x1, blocking collectives, chan_sum(): got = lax.all_to_all(pieces, axis, 0, 0, tiled=False)  17 us
    all_to_all x1, blocking collectives, chan_sum(): back = lax.all_to_all(rep, axis, 0, 0, tiled=False)  12.7 us
    dot_general x1, matrix products, cut_windows(): jnp.einsum('bkips,bcs->ibkpc', hot, blocks, preferred_element_type=jnp.fl...  11.9 us
    all_to_all x1, starting transfers between devices, scatter_owners(): got = lax.all_to_all(pieces, axis, 0, 0, tiled=False)  10.1 us
    conv_general_dilated x7, local copies, waits for them, and re-layouts, correlate(): lax.conv_general_dilated(extended[None], weights, (1,), 'VALID', rhs_dila...  8.38 us
    all_to_all x1, starting transfers between devices, gather_blocks(): recv = lax.all_to_all(rep, axis, 0, 0, tiled=False)  7.49 us
    all_to_all x1, waiting for transfers between devices, scatter_owners(): got = lax.all_to_all(pieces, axis, 0, 0, tiled=False)  6.91 us
  transfers between devices with their start and end apart: 3, of which 2 were waited for; matrix products, arithmetic and copies ran while one was open for 8% of the time, Pallas kernels for 0%

profile of v5, /device:TPU:1, one launch (start us, length us, event | category | flops | bytes accessed | tf_op | source)
XLA Modules:
  0.0 162.1 jit_solution(16992725746169876724)
XLA Ops:
  0.0 1.8 %reshape.161 = bf16[4,80,4,256]{3,2,1,0:T(4,128)(2,1)S(1)} reshape(bf16[320,1024]{1,0:T(8,128)(2,1)} %param.9) | data formatting | bytes 1310720 | tf_op jit(solution)/shard_map/reshape | solution.py:22
  1.8 0.9 copy.33
  2.8 10.1 %all-to-all-start = ((bf16[16,80,256]{2,1,0:T(8,128)(2,1)}), bf16[16,80,256]{2,1,0:T(8,128)(2,1)S(1)}, u32[]{:S(2)}, u32[]{:S(2)}) async-start(bf16[16,80,256]{2,1,0:T(8,128)(2,1)} %bitcast.1), calls=%async_computation | async-start | bytes 1310720 | tf_op jit(solution)/shard_map/all_to_all | solution.py:36
  12.9 0.9 slice.103
  13.8 1.3 collective-permute-start
  15.1 0.6 fusion.29
  23.3 6.9 %all-to-all-done = bf16[16,80,256]{2,1,0:T(8,128)(2,1)S(1)} async-done(((bf16[16,80,256]{2,1,0:T(8,128)(2,1)}), bf16[16,80,256]{2,1,0:T(8,128)(2,1)S(1)}, u32[]{:S(2)}, u32[]{:S(2)}) %all-to-all-start) | async-done | bytes 655392 | tf_op jit(solution)/shard_map/all_to_all | solution.py:36
  30.3 1.8 %broadcast_in_dim.17 = bf16[16,4,80,256]{3,2,1,0:T(8,128)(2,1)} broadcast(bf16[4,80,256]{2,1,0:T(8,128)(2,1)S(1)} %pad_maximum_fusion), dimensions={1,2,3} | broadcast | bytes 2785280 | tf_op jit(solution)/shard_map/broadcast_in_dim | solution.py:42
  32.0 7.5 %all-to-all-start.1 = ((bf16[16,4,80,256]{3,2,1,0:T(8,128)(2,1)}), bf16[16,4,80,256]{3,2,1,0:T(8,128)(2,1)S(1)}, u32[]{:S(2)}, u32[]{:S(2)}) async-start(bf16[16,4,80,256]{3,2,1,0:T(8,128)(2,1)} %broadcast_in_dim.17), calls=%async_computation.1 | async-start | bytes 5242880 | tf_op jit(solution)/shard_map/all_to_all | solution.py:43
  39.6 1.1 constant_dynamic-update-slice_fusion.1
  40.7 0.8 broadcast_add_fusion
  42.1 0.9 pad.12
  43.0 3.8 %reshape.189 = bf16[320,1,8,141]{3,2,0,1:T(8,128)(2,1)} reshape(bf16[320,1,1128]{2,0,1:T(8,128)(2,1)} %pad.12) | data formatting | bytes 1443840 | tf_op jit(solution)/shard_map/conv_general_dilated | solution.py:79
  46.8 2.7 %copy.36 = bf16[320,1,8,141]{0,2,3,1:T(8,128)(2,1)S(1)} copy(bf16[320,1,8,141]{3,2,0,1:T(8,128)(2,1)} %reshape.189) | data formatting | bytes 1443840 | tf_op jit(solution)/shard_map/conv_general_dilated | solution.py:79
  49.5 1.0 slice.122
  50.7 49.7 %all-to-all-done.1 = bf16[16,4,80,256]{3,2,1,0:T(8,128)(2,1)S(1)} async-done(((bf16[16,4,80,256]{3,2,1,0:T(8,128)(2,1)}), bf16[16,4,80,256]{3,2,1,0:T(8,128)(2,1)S(1)}, u32[]{:S(2)}, u32[]{:S(2)}) %all-to-all-start.1) | async-done | bytes 2621472 | tf_op jit(solution)/shard_map/all_to_all | solution.py:43
  101.0 3.5 %copy.37 = bf16[4,4,80,4,256]{4,3,2,1,0:T(4,128)(2,1)} copy(bf16[4,4,80,4,256]{4,2,0,3,1:T(8,128)(2,1)S(1)} %bitcast.54) | data formatting | bytes 5242880 | tf_op jit(solution)/shard_map/transpose | solution.py:31
  104.5 4.2 %reshape.187 = bf16[4,320,1024,1,1]{2,1,0,3,4:T(8,128)(2,1)S(1)} reshape(bf16[4,4,80,4,256]{4,3,2,1,0:T(4,128)(2,1)} %copy.37) | data formatting | bytes 5242880 | tf_op jit(solution)/shard_map/reshape | solution.py:31
  109.1 11.9 %fusion.7 = bf16[4,320,16,25,4]{1,3,4,2,0:T(8,128)(2,1)S(1)} fusion(s32[4,16,25,4]{2,3,1,0:T(4,128)} %broadcast_add_fusion, pred[25,4]{0,1:T(4,128)(4,1)S(1)} %broadcast_compare_fusion, bf16[4,320,1024,1,1]{2,1,0,3,4:T(8,128)(2,1)S(1)} %reshape.187), kind=kOutput, calls=%fused_computation.8 | convolution fusion | flops 4209459200 | bytes 6743140 | tf_op jit(solution)/shard_map/bkips,bcs->ibkpc/dot_general | solution.py:55
  121.0 6.3 %fusion.18 = f32[8,141,256]{2,0,1:T(8,128)S(1)} fusion(bf16[25,256,320]{2,0,1:T(8,128)(2,1)S(1)} %bitcast.70, bf16[320,1,7,96]{0,2,3,1:T(8,128)(2,1)S(1)} %copy-done, bf16[320,1,8,141]{0,2,3,1:T(8,128)(2,1)S(1)} %copy.36, pred[8,141]{0,1:T(8,128)(4,1)S(1)} %copy-done.3), kind=kOutput, calls=%fused_computation.18 | convolution fusion | flops 4624217088 | bytes 6404200 | tf_op jit(solution)/shard_map/conv_general_dilated | solution.py:79
  128.6 2.2 %slice_add_fusion = f32[64,1,1024]{2,1,0:T(1,128)S(1)} fusion(f32[64,4,1027]{2,1,0:T(4,128)S(1)} %reshape_squeeze.3), kind=kLoop, calls=%fused_computation.23 | loop fusion | flops 196608 | bytes 1310720 | tf_op jit(solution)/shard_map/add | solution.py:86
  131.4 17.0 %all_to_all.20 = f32[16,40,128]{2,1,0:T(8,128)S(1)} all-to-all(f32[16,40,128]{2,1,0:T(8,128)S(1)} %bitcast.59), channel_id=1, replica_groups=mesh['tm'=16,'chan'=16] {'chan'}, dimensions={0} | all-to-all | bytes 655360 | tf_op jit(solution)/shard_map/all_to_all | solution.py:71
  148.5 12.7 %all_to_all.21 = f32[16,40,128]{2,1,0:T(8,128)S(1)} all-to-all(f32[16,40,128]{2,1,0:T(8,128)S(1)} %broadcast_in_dim.25), channel_id=1, replica_groups=mesh['tm'=16,'chan'=16] {'chan'}, dimensions={0} | all-to-all | bytes 655360 | tf_op jit(solution)/shard_map/all_to_all | solution.py:74
  161.3 0.8 slice_multiply_fusion
  (43 shorter events, 3.8 us)
Async XLA Ops:
  0.0 15.1 %copy-start.2 = (s32[4]{0:T(128)S(1)}, s32[4]{0:T(128)}, u32[]{:S(2)}) copy-start(s32[4]{0:T(128)} %param.10) | copy-start | bytes 52
  2.8 27.5 %all-to-all-start = ((bf16[16,80,256]{2,1,0:T(8,128)(2,1)}), bf16[16,80,256]{2,1,0:T(8,128)(2,1)S(1)}, u32[]{:S(2)}, u32[]{:S(2)}) async-start(bf16[16,80,256]{2,1,0:T(8,128)(2,1)} %bitcast.1), calls=%async_computation | async-start | bytes 1310720 | tf_op jit(solution)/shard_map/all_to_all | solution.py:36
  13.8 16.5 %collective-permute-start = (bf16[320,99]{1,0:T(8,128)(2,1)S(1)}, bf16[320,99]{1,0:T(8,128)(2,1)S(1)}, u32[]{:S(2)}, u32[]{:S(2)}) collective-permute-start(bf16[320,99]{1,0:T(8,128)(2,1)S(1)} %slice.103), channel_id=1, source_target_pairs={{16,0},{32,16},{48,32},{64,48},{80,64},{96,80},{112,96},{128,112},... | collective-permute-start | bytes 190088 | tf_op jit(solution)/shard_map/ppermute | solution.py:16
  32.0 8.7 %copy-start.1 = (s32[4,16]{1,0:T(4,128)S(1)}, s32[4,16]{1,0:T(4,128)}, u32[]{:S(2)}) copy-start(s32[4,16]{1,0:T(4,128)} %param.11) | copy-start | bytes 772
  32.0 68.4 %all-to-all-start.1 = ((bf16[16,4,80,256]{3,2,1,0:T(8,128)(2,1)}), bf16[16,4,80,256]{3,2,1,0:T(8,128)(2,1)S(1)}, u32[]{:S(2)}, u32[]{:S(2)}) async-start(bf16[16,4,80,256]{3,2,1,0:T(8,128)(2,1)} %broadcast_in_dim.17), calls=%async_computation.1 | async-start | bytes 5242880 | tf_op jit(solution)/shard_map/all_to_all | solution.py:43
  109.1 11.9 %copy-start = (bf16[320,1,7,96]{0,2,3,1:T(8,128)(2,1)S(1)}, bf16[320,1,7,96]{0,2,3,1:T(8,128)(2,1)}, u32[]{:S(2)}) copy-start(bf16[320,1,7,96]{0,2,3,1:T(8,128)(2,1)} %slice.122) | copy-start | bytes 1290244
  109.1 11.9 %copy-start.3 = (pred[8,141]{0,1:T(8,128)(4,1)S(1)}, pred[8,141]{0,1:T(8,128)(4,1)}, u32[]{:S(2)}) copy-start(pred[8,141]{0,1:T(8,128)(4,1)} %constant.118) | copy-start | bytes 3388

commit v6 on v5

--- a/solution.py
+++ b/solution.py
@@ -6,7 +6,7 @@
 L = 100
 PHASES = 4
 STAGES = 1
-BLOCK_GRID = (4, 4)
+BLOCK_GRID = (2, 8)
 SUM_GRID = (2, 8)
 
 

time: 163 us -> 162 us (level)
    reshape x2 -> x1, local copies, waits for them, and re-layouts: 1.88 us -> 0.07 us  [dense_pieces(): grid = block.reshape(across[0], down, across[1], wide)]
where the time goes in v6:
time: 162 us; the launch traced here: 161 us
  waiting for transfers between devices  56.7 us (35%)
  blocking collectives  29.7 us (18%)
  local copies, waits for them, and re-layouts  24.6 us (15%)
  starting transfers between devices  18.9 us (12%)
  matrix products  18.2 us (11%)
  between operations  7.86 us (5%)
  other arithmetic  5.26 us (3%)
    all_to_all x1, waiting for transfers between devices, gather_blocks(): recv = lax.all_to_all(rep, axis, 0, 0, tiled=False)  49.7 us
    all_to_all x1, blocking collectives, chan_sum(): got = lax.all_to_all(pieces, axis, 0, 0, tiled=False)  17 us
    all_to_all x1, blocking collectives, chan_sum(): back = lax.all_to_all(rep, axis, 0, 0, tiled=False)  12.7 us
    dot_general x1, matrix products, cut_windows(): jnp.einsum('bkips,bcs->ibkpc', hot, blocks, preferred_element_type=jnp.fl...  11.9 us
    all_to_all x1, starting transfers between devices, scatter_owners(): got = lax.all_to_all(pieces, axis, 0, 0, tiled=False)  10.1 us
    conv_general_dilated x7, local copies, waits for them, and re-layouts, correlate(): lax.conv_general_dilated(extended[None], weights, (1,), 'VALID', rhs_dila...  8.38 us
    all_to_all x1, starting transfers between devices, gather_blocks(): recv = lax.all_to_all(rep, axis, 0, 0, tiled=False)  7.49 us
    all_to_all x1, waiting for transfers between devices, scatter_owners(): got = lax.all_to_all(pieces, axis, 0, 0, tiled=False)  6.91 us
  transfers between devices with their start and end apart: 3, of which 2 were waited for; matrix products, arithmetic and copies ran while one was open for 8% of the time, Pallas kernels for 0%

profile of v6, /device:TPU:1, one launch (start us, length us, event | category | flops | bytes accessed | tf_op | source)
XLA Modules:
  0.0 161.1 jit_solution(771749705504358300)
XLA Ops:
  0.0 1.2 copy.47
  1.3 0.9 copy.33
  2.2 10.1 %all-to-all-start = ((bf16[16,160,128]{2,1,0:T(8,128)(2,1)}), bf16[16,160,128]{2,1,0:T(8,128)(2,1)S(1)}, u32[]{:S(2)}, u32[]{:S(2)}) async-start(bf16[16,160,128]{2,1,0:T(8,128)(2,1)} %bitcast.1), calls=%async_computation | async-start | bytes 1310720 | tf_op jit(solution)/shard_map/all_to_all | solution.py:36
  12.3 0.9 slice.103
  13.2 1.3 collective-permute-start
  14.5 0.6 fusion.29
  22.8 6.9 %all-to-all-done = bf16[16,160,128]{2,1,0:T(8,128)(2,1)S(1)} async-done(((bf16[16,160,128]{2,1,0:T(8,128)(2,1)}), bf16[16,160,128]{2,1,0:T(8,128)(2,1)S(1)}, u32[]{:S(2)}, u32[]{:S(2)}) %all-to-all-start) | async-done | bytes 655392 | tf_op jit(solution)/shard_map/all_to_all | solution.py:36
  29.7 2.0 %broadcast_in_dim.17 = bf16[16,4,160,128]{3,2,1,0:T(8,128)(2,1)} broadcast(bf16[4,160,128]{2,1,0:T(8,128)(2,1)S(1)} %pad_maximum_fusion), dimensions={1,2,3} | broadcast | bytes 2785280 | tf_op jit(solution)/shard_map/broadcast_in_dim | solution.py:42
  31.7 7.5 %all-to-all-start.1 = ((bf16[16,4,160,128]{3,2,1,0:T(8,128)(2,1)}), bf16[16,4,160,128]{3,2,1,0:T(8,128)(2,1)S(1)}, u32[]{:S(2)}, u32[]{:S(2)}) async-start(bf16[16,4,160,128]{3,2,1,0:T(8,128)(2,1)} %broadcast_in_dim.17), calls=%async_computation.1 | async-start | bytes 5242880 | tf_op jit(solution)/shard_map/all_to_all | solution.py:43
  39.3 1.1 constant_dynamic-update-slice_fusion.1
  40.4 0.8 broadcast_add_fusion
  41.8 0.9 pad.12
  42.7 3.8 %reshape.189 = bf16[320,1,8,141]{3,2,0,1:T(8,128)(2,1)} reshape(bf16[320,1,1128]{2,0,1:T(8,128)(2,1)} %pad.12) | data formatting | bytes 1443840 | tf_op jit(solution)/shard_map/conv_general_dilated | solution.py:79
  46.5 2.7 %copy.36 = bf16[320,1,8,141]{0,2,3,1:T(8,128)(2,1)S(1)} copy(bf16[320,1,8,141]{3,2,0,1:T(8,128)(2,1)} %reshape.189) | data formatting | bytes 1443840 | tf_op jit(solution)/shard_map/conv_general_dilated | solution.py:79
  49.2 1.0 slice.122
  50.4 49.7 %all-to-all-done.1 = bf16[16,4,160,128]{3,2,1,0:T(8,128)(2,1)S(1)} async-done(((bf16[16,4,160,128]{3,2,1,0:T(8,128)(2,1)}), bf16[16,4,160,128]{3,2,1,0:T(8,128)(2,1)S(1)}, u32[]{:S(2)}, u32[]{:S(2)}) %all-to-all-start.1) | async-done | bytes 2621472 | tf_op jit(solution)/shard_map/all_to_all | solution.py:43
  100.7 3.2 %copy.37 = bf16[4,2,160,8,128]{4,3,2,1,0:T(8,128)(2,1)} copy(bf16[4,2,160,8,128]{4,2,0,3,1:T(8,128)(2,1)S(1)} %bitcast.62) | data formatting | bytes 5242880 | tf_op jit(solution)/shard_map/transpose | solution.py:31
  103.9 3.8 %reshape.187 = bf16[4,320,1024,1,1]{2,1,0,3,4:T(8,128)(2,1)S(1)} reshape(bf16[4,2,160,8,128]{4,3,2,1,0:T(8,128)(2,1)} %copy.37) | data formatting | bytes 5242880 | tf_op jit(solution)/shard_map/reshape | solution.py:31
  108.0 11.9 %fusion.7 = bf16[4,320,16,25,4]{1,3,4,2,0:T(8,128)(2,1)S(1)} fusion(s32[4,16,25,4]{2,3,1,0:T(4,128)} %broadcast_add_fusion, pred[25,4]{0,1:T(4,128)(4,1)S(1)} %broadcast_compare_fusion, bf16[4,320,1024,1,1]{2,1,0,3,4:T(8,128)(2,1)S(1)} %reshape.187), kind=kOutput, calls=%fused_computation.8 | convolution fusion | flops 4209459200 | bytes 6743140 | tf_op jit(solution)/shard_map/bkips,bcs->ibkpc/dot_general | solution.py:55
  119.9 6.3 %fusion.18 = f32[8,141,256]{2,0,1:T(8,128)S(1)} fusion(bf16[25,256,320]{2,0,1:T(8,128)(2,1)S(1)} %bitcast.79, bf16[320,1,7,96]{0,2,3,1:T(8,128)(2,1)S(1)} %copy-done, bf16[320,1,8,141]{0,2,3,1:T(8,128)(2,1)S(1)} %copy.36, pred[8,141]{0,1:T(8,128)(4,1)S(1)} %copy-done.3), kind=kOutput, calls=%fused_computation.18 | convolution fusion | flops 4624217088 | bytes 6404200 | tf_op jit(solution)/shard_map/conv_general_dilated | solution.py:79
  127.5 2.2 %slice_add_fusion = f32[64,1,1024]{2,1,0:T(1,128)S(1)} fusion(f32[64,4,1027]{2,1,0:T(4,128)S(1)} %reshape_squeeze.3), kind=kLoop, calls=%fused_computation.24 | loop fusion | flops 196608 | bytes 1310720 | tf_op jit(solution)/shard_map/add | solution.py:86
  130.4 17.0 %all_to_all.20 = f32[16,40,128]{2,1,0:T(8,128)S(1)} all-to-all(f32[16,40,128]{2,1,0:T(8,128)S(1)} %bitcast.68), channel_id=1, replica_groups=mesh['tm'=16,'chan'=16] {'chan'}, dimensions={0} | all-to-all | bytes 655360 | tf_op jit(solution)/shard_map/all_to_all | solution.py:71
  147.4 12.7 %all_to_all.21 = f32[16,40,128]{2,1,0:T(8,128)S(1)} all-to-all(f32[16,40,128]{2,1,0:T(8,128)S(1)} %broadcast_in_dim.25), channel_id=1, replica_groups=mesh['tm'=16,'chan'=16] {'chan'}, dimensions={0} | all-to-all | bytes 655360 | tf_op jit(solution)/shard_map/all_to_all | solution.py:74
  160.3 0.8 slice_multiply_fusion
  (44 shorter events, 3.8 us)
Async XLA Ops:
  0.0 14.5 %copy-start.2 = (s32[4]{0:T(128)S(1)}, s32[4]{0:T(128)}, u32[]{:S(2)}) copy-start(s32[4]{0:T(128)} %param.10) | copy-start | bytes 52
  2.2 27.5 %all-to-all-start = ((bf16[16,160,128]{2,1,0:T(8,128)(2,1)}), bf16[16,160,128]{2,1,0:T(8,128)(2,1)S(1)}, u32[]{:S(2)}, u32[]{:S(2)}) async-start(bf16[16,160,128]{2,1,0:T(8,128)(2,1)} %bitcast.1), calls=%async_computation | async-start | bytes 1310720 | tf_op jit(solution)/shard_map/all_to_all | solution.py:36
  13.2 16.5 %collective-permute-start = (bf16[320,99]{1,0:T(8,128)(2,1)S(1)}, bf16[320,99]{1,0:T(8,128)(2,1)S(1)}, u32[]{:S(2)}, u32[]{:S(2)}) collective-permute-start(bf16[320,99]{1,0:T(8,128)(2,1)S(1)} %slice.103), channel_id=1, source_target_pairs={{16,0},{32,16},{48,32},{64,48},{80,64},{96,80},{112,96},{128,112},... | collective-permute-start | bytes 190088 | tf_op jit(solution)/shard_map/ppermute | solution.py:16
  31.7 8.7 %copy-start.1 = (s32[4,16]{1,0:T(4,128)S(1)}, s32[4,16]{1,0:T(4,128)}, u32[]{:S(2)}) copy-start(s32[4,16]{1,0:T(4,128)} %param.11) | copy-start | bytes 772
  31.7 68.4 %all-to-all-start.1 = ((bf16[16,4,160,128]{3,2,1,0:T(8,128)(2,1)}), bf16[16,4,160,128]{3,2,1,0:T(8,128)(2,1)S(1)}, u32[]{:S(2)}, u32[]{:S(2)}) async-start(bf16[16,4,160,128]{3,2,1,0:T(8,128)(2,1)} %broadcast_in_dim.17), calls=%async_computation.1 | async-start | bytes 5242880 | tf_op jit(solution)/shard_map/all_to_all | solution.py:43
  108.0 11.9 %copy-start = (bf16[320,1,7,96]{0,2,3,1:T(8,128)(2,1)S(1)}, bf16[320,1,7,96]{0,2,3,1:T(8,128)(2,1)}, u32[]{:S(2)}) copy-start(bf16[320,1,7,96]{0,2,3,1:T(8,128)(2,1)} %slice.122) | copy-start | bytes 1290244
  108.0 11.9 %copy-start.3 = (pred[8,141]{0,1:T(8,128)(4,1)S(1)}, pred[8,141]{0,1:T(8,128)(4,1)}, u32[]{:S(2)}) copy-start(pred[8,141]{0,1:T(8,128)(4,1)} %constant.118) | copy-start | bytes 3388

commit v7 on v6

--- a/solution.py
+++ b/solution.py
@@ -52,7 +52,7 @@
     idx = offsets[:, :, None, None] + lag[None, None]
     hot = (jnp.arange(samples, dtype=offsets.dtype) == idx[..., None]) & (lag[None, None, :, :, None] < taps)
     hot = hot.astype(blocks.dtype)
-    cut = jnp.einsum("bkips,bcs->ibkpc", hot, blocks, preferred_element_type=jnp.float32).astype(blocks.dtype)
+    cut = jnp.einsum("bcs,bkips->ibkpc", blocks, hot, preferred_element_type=jnp.float32).astype(blocks.dtype)
     return cut.reshape(steps, batches * per_batch * phases, width)
 
 
@@ -94,9 +94,11 @@
     templates = batches * per_batch
     phases = PHASES
     span = -(-taps // phases) * phases
-    rim = from_behind(record[:, : taps - 1], "tm", -1)
+    lane = 128
+    rim = from_behind(record[:, : -(-(taps - 1) // lane) * lane], "tm", -1)
     sel = scatter_owners(record, owner, "tm")
     rim, sel = lax.optimization_barrier((rim, sel))
+    rim = rim[:, : taps - 1]
     extended = jnp.concatenate(
         [record, rim, jnp.zeros((width, span - taps), record.dtype)], axis=1
     )

time: 162 us -> 161 us (level)
  transfers between devices with their start and end apart: 3 -> 3, of which waited for: 2 -> 2; matrix products, arithmetic and copies ran while one was open for 8% -> 7% of each run, Pallas kernels for 0% -> 0%
where the time goes in v7:
time: 161 us; the launch traced here: 160 us
  waiting for transfers between devices  57.8 us (36%)
  blocking collectives  29.7 us (18%)
  local copies, waits for them, and re-layouts  24 us (15%)
  starting transfers between devices  18.9 us (12%)
  matrix products  17.3 us (11%)
  between operations  7.89 us (5%)
  other arithmetic  4.66 us (3%)
    all_to_all x1, waiting for transfers between devices, gather_blocks(): recv = lax.all_to_all(rep, axis, 0, 0, tiled=False)  50.1 us
    all_to_all x1, blocking collectives, chan_sum(): got = lax.all_to_all(pieces, axis, 0, 0, tiled=False)  17 us
    all_to_all x1, blocking collectives, chan_sum(): back = lax.all_to_all(rep, axis, 0, 0, tiled=False)  12.7 us
    dot_general x1, matrix products, cut_windows(): jnp.einsum('bcs,bkips->ibkpc', blocks, hot, preferred_element_type=jnp.fl...  10.9 us
    all_to_all x1, starting transfers between devices, scatter_owners(): got = lax.all_to_all(pieces, axis, 0, 0, tiled=False)  10.1 us
    conv_general_dilated x7, local copies, waits for them, and re-layouts, correlate(): lax.conv_general_dilated(extended[None], weights, (1,), 'VALID', rhs_dila...  9.82 us
    all_to_all x1, waiting for transfers between devices, scatter_owners(): got = lax.all_to_all(pieces, axis, 0, 0, tiled=False)  7.75 us
    all_to_all x1, starting transfers between devices, gather_blocks(): recv = lax.all_to_all(rep, axis, 0, 0, tiled=False)  7.49 us
  transfers between devices with their start and end apart: 3, of which 2 were waited for; matrix products, arithmetic and copies ran while one was open for 7% of the time, Pallas kernels for 0%

profile of v7, /device:TPU:1, one launch (start us, length us, event | category | flops | bytes accessed | tf_op | source)
XLA Modules:
  0.0 160.3 jit_solution(5305307981435579986)
XLA Ops:
  0.0 1.3 copy.47
  1.3 0.9 copy.33
  2.3 10.1 %all-to-all-start = ((bf16[16,160,128]{2,1,0:T(8,128)(2,1)}), bf16[16,160,128]{2,1,0:T(8,128)(2,1)S(1)}, u32[]{:S(2)}, u32[]{:S(2)}) async-start(bf16[16,160,128]{2,1,0:T(8,128)(2,1)} %bitcast.1), calls=%async_computation | async-start | bytes 1310720 | tf_op jit(solution)/shard_map/all_to_all | solution.py:36
  12.4 1.3 collective-permute-start
  13.7 0.6 fusion.30
  22.0 7.8 %all-to-all-done = bf16[16,160,128]{2,1,0:T(8,128)(2,1)S(1)} async-done(((bf16[16,160,128]{2,1,0:T(8,128)(2,1)}), bf16[16,160,128]{2,1,0:T(8,128)(2,1)S(1)}, u32[]{:S(2)}, u32[]{:S(2)}) %all-to-all-start) | async-done | bytes 655392 | tf_op jit(solution)/shard_map/all_to_all | solution.py:36
  29.8 2.0 %broadcast_in_dim.17 = bf16[16,4,160,128]{3,2,1,0:T(8,128)(2,1)} broadcast(bf16[4,160,128]{2,1,0:T(8,128)(2,1)S(1)} %pad_maximum_fusion.1), dimensions={1,2,3} | broadcast | bytes 2785280 | tf_op jit(solution)/shard_map/broadcast_in_dim | solution.py:42
  31.8 7.5 %all-to-all-start.1 = ((bf16[16,4,160,128]{3,2,1,0:T(8,128)(2,1)}), bf16[16,4,160,128]{3,2,1,0:T(8,128)(2,1)S(1)}, u32[]{:S(2)}, u32[]{:S(2)}) async-start(bf16[16,4,160,128]{3,2,1,0:T(8,128)(2,1)} %broadcast_in_dim.17), calls=%async_computation.1 | async-start | bytes 5242880 | tf_op jit(solution)/shard_map/all_to_all | solution.py:43
  40.1 0.9 pad.12
  41.0 3.8 %reshape.189 = bf16[320,1,8,141]{3,2,0,1:T(8,128)(2,1)} reshape(bf16[320,1,1128]{2,0,1:T(8,128)(2,1)} %pad.12) | data formatting | bytes 1443840 | tf_op jit(solution)/shard_map/conv_general_dilated | solution.py:79
  44.8 3.0 %copy.36 = bf16[320,1,8,141]{0,2,3,1:T(8,128)(2,1)} copy(bf16[320,1,8,141]{3,2,0,1:T(8,128)(2,1)} %reshape.189) | data formatting | bytes 1443840 | tf_op jit(solution)/shard_map/conv_general_dilated | solution.py:79
  47.9 2.0 %slice.126 = bf16[320,1,7,96]{0,2,3,1:T(8,128)(2,1)} slice(bf16[320,1,8,141]{0,2,3,1:T(8,128)(2,1)} %copy.36), slice={[0:320], [0:1], [1:8], [0:96]} | slice | bytes 860160 | tf_op jit(solution)/shard_map/conv_general_dilated | solution.py:79
  50.2 50.1 %all-to-all-done.1 = bf16[16,4,160,128]{3,2,1,0:T(8,128)(2,1)S(1)} async-done(((bf16[16,4,160,128]{3,2,1,0:T(8,128)(2,1)}), bf16[16,4,160,128]{3,2,1,0:T(8,128)(2,1)S(1)}, u32[]{:S(2)}, u32[]{:S(2)}) %all-to-all-start.1) | async-done | bytes 2621472 | tf_op jit(solution)/shard_map/all_to_all | solution.py:43
  100.2 0.5 multiply_reduce_fusion
  100.8 3.2 %copy.37 = bf16[4,2,160,8,128]{4,3,2,1,0:T(8,128)(2,1)} copy(bf16[4,2,160,8,128]{4,2,0,3,1:T(8,128)(2,1)S(1)} %bitcast.64) | data formatting | bytes 5242880 | tf_op jit(solution)/shard_map/transpose | solution.py:31
  104.0 3.8 %reshape.187 = bf16[4,320,1024,1,1]{2,1,0,3,4:T(8,128)(2,1)S(1)} reshape(bf16[4,2,160,8,128]{4,3,2,1,0:T(8,128)(2,1)} %copy.37) | data formatting | bytes 5242880 | tf_op jit(solution)/shard_map/reshape | solution.py:31
  108.1 10.9 %fusion.7 = bf16[4,16,25,4,320]{4,2,3,1,0:T(8,128)(2,1)S(1)} fusion(s32[4,16,25,4]{2,3,1,0:T(4,128)S(1)} %broadcast_add_fusion, pred[25,4]{0,1:T(4,128)(4,1)S(1)} %broadcast_compare_fusion, bf16[4,320,1024,1,1]{2,1,0,3,4:T(8,128)(2,1)S(1)} %reshape.187), kind=kOutput, calls=%fused_computation.8 | convolution fusion | flops 4209459200 | bytes 6743140 | tf_op jit(solution)/shard_map/bcs,bkips->ibkpc/dot_general | solution.py:55
  119.1 6.4 %fusion.18 = f32[8,141,256]{2,0,1:T(8,128)S(1)} fusion(bf16[25,256,320]{2,0,1:T(8,128)(2,1)S(1)} %bitcast.82, bf16[320,1,7,96]{0,2,3,1:T(8,128)(2,1)S(1)} %copy-done.2, bf16[320,1,8,141]{0,2,3,1:T(8,128)(2,1)S(1)} %copy-done.1, pred[8,141]{0,1:T(8,128)(4,1)S(1)} %copy-done.5), kind=kOutput, calls=%fused_computation.18 | convolution fusion | flops 4624217088 | bytes 6404200 | tf_op jit(solution)/shard_map/conv_general_dilated | solution.py:79
  125.4 0.4 copy.39
  126.1 0.4 copy.40
  126.8 2.2 %slice_add_fusion = f32[64,1,1024]{2,1,0:T(1,128)S(1)} fusion(f32[64,4,1027]{2,1,0:T(4,128)S(1)} %reshape_squeeze.3), kind=kLoop, calls=%fused_computation.26 | loop fusion | flops 196608 | bytes 1310720 | tf_op jit(solution)/shard_map/add | solution.py:86
  129.6 17.0 %all_to_all.20 = f32[16,40,128]{2,1,0:T(8,128)S(1)} all-to-all(f32[16,40,128]{2,1,0:T(8,128)S(1)} %bitcast.69), channel_id=1, replica_groups=mesh['tm'=16,'chan'=16] {'chan'}, dimensions={0} | all-to-all | bytes 655360 | tf_op jit(solution)/shard_map/all_to_all | solution.py:71
  146.7 12.7 %all_to_all.21 = f32[16,40,128]{2,1,0:T(8,128)S(1)} all-to-all(f32[16,40,128]{2,1,0:T(8,128)S(1)} %broadcast_in_dim.25), channel_id=1, replica_groups=mesh['tm'=16,'chan'=16] {'chan'}, dimensions={0} | all-to-all | bytes 655360 | tf_op jit(solution)/shard_map/all_to_all | solution.py:74
  159.5 0.8 slice_multiply_fusion
  (47 shorter events, 2.7 us)
Async XLA Ops:
  0.0 12.4 %copy-start = (bf16[320,1024]{1,0:T(8,128)(2,1)S(1)}, bf16[320,1024]{1,0:T(8,128)(2,1)}, u32[]{:S(2)}) copy-start(bf16[320,1024]{1,0:T(8,128)(2,1)} %param.9) | copy-start | bytes 1966084
  0.0 13.7 %copy-start.4 = (s32[4]{0:T(128)S(1)}, s32[4]{0:T(128)}, u32[]{:S(2)}) copy-start(s32[4]{0:T(128)} %param.10) | copy-start | bytes 52
  2.3 27.5 %all-to-all-start = ((bf16[16,160,128]{2,1,0:T(8,128)(2,1)}), bf16[16,160,128]{2,1,0:T(8,128)(2,1)S(1)}, u32[]{:S(2)}, u32[]{:S(2)}) async-start(bf16[16,160,128]{2,1,0:T(8,128)(2,1)} %bitcast.1), calls=%async_computation | async-start | bytes 1310720 | tf_op jit(solution)/shard_map/all_to_all | solution.py:36
  12.4 17.3 %collective-permute-start = (bf16[320,128]{1,0:T(8,128)(2,1)S(1)}, bf16[320,128]{1,0:T(8,128)(2,1)S(1)}, u32[]{:S(2)}, u32[]{:S(2)}) collective-permute-start(bf16[320,128]{1,0:T(8,128)(2,1)S(1)} %slice.106), channel_id=1, source_target_pairs={{16,0},{32,16},{48,32},{64,48},{80,64},{96,80},{112,96},{128,112},... | collective-permute-start | bytes 245768 | tf_op jit(solution)/shard_map/ppermute | solution.py:16
  31.8 7.5 %copy-start.3 = (s32[4,16]{1,0:T(4,128)S(1)}, s32[4,16]{1,0:T(4,128)}, u32[]{:S(2)}) copy-start(s32[4,16]{1,0:T(4,128)} %param.11) | copy-start | bytes 772
  31.8 68.4 %all-to-all-start.1 = ((bf16[16,4,160,128]{3,2,1,0:T(8,128)(2,1)}), bf16[16,4,160,128]{3,2,1,0:T(8,128)(2,1)S(1)}, u32[]{:S(2)}, u32[]{:S(2)}) async-start(bf16[16,4,160,128]{3,2,1,0:T(8,128)(2,1)} %broadcast_in_dim.17), calls=%async_computation.1 | async-start | bytes 5242880 | tf_op jit(solution)/shard_map/all_to_all | solution.py:43
  108.1 11.0 %copy-start.1 = (bf16[320,1,8,141]{0,2,3,1:T(8,128)(2,1)S(1)}, bf16[320,1,8,141]{0,2,3,1:T(8,128)(2,1)}, u32[]{:S(2)}) copy-start(bf16[320,1,8,141]{0,2,3,1:T(8,128)(2,1)} %copy.36) | copy-start | bytes 2165764
  108.1 11.0 %copy-start.2 = (bf16[320,1,7,96]{0,2,3,1:T(8,128)(2,1)S(1)}, bf16[320,1,7,96]{0,2,3,1:T(8,128)(2,1)}, u32[]{:S(2)}) copy-start(bf16[320,1,7,96]{0,2,3,1:T(8,128)(2,1)} %slice.126) | copy-start | bytes 1290244
  108.1 11.0 %copy-start.5 = (pred[8,141]{0,1:T(8,128)(4,1)S(1)}, pred[8,141]{0,1:T(8,128)(4,1)}, u32[]{:S(2)}) copy-start(pred[8,141]{0,1:T(8,128)(4,1)} %constant.118) | copy-start | bytes 3388
